TPU v7x, 128 devices: a whole 4x4x4 slice. The times are simulated.
128 devices in a mesh: det: 8 (over x, core), tm: 16 (over z, y).
Axes of the slice: x: 4, y: 4, z: 4, core: 2. Of those that a mesh axis runs over, the one named last changes fastest.
Arguments:
- samples: float32 [32, 1024, 128], P('det', 'tm'), may hold values from -6 to 6
- pointing: bfloat16 [32, 1024, 128, 128], P('det', 'tm'), may hold values from -0.25 to 0.25
- pix_block: int32 [32, 1024], P('det', 'tm'), may hold values from 0 to 8191, as said below
- det_weight: float32 [32], P('det'), may hold values from 0.5 to 2
- start_map: float32 [128, 8192], P(('det', 'tm')), may hold values from -6 to 6
- legendre: bfloat16 [1024, 6144, 128], P(('det', 'tm')), may hold values from -0.5 to 0.5
- prior_gain: float32 [6144], replicated, may hold values from 0.3 to 3
- m_values: int32 [1024], replicated, may hold values from 0 to 4095, as said below
- cycle_offset: int32 [128], P(('det', 'tm')), may hold values from 0 to 8191
Outputs:
- final_map: float32 [128, 8192], P(('det', 'tm'))
Inputs may be any that keep to these rules, and one draw needn't show every extreme that they name: `m_values`: strictly increasing; entry k lies in k * 4 to (k + 1) * 4 - 1, the first is 0 and the last is 4095. `pix_block`: the cycle owner of block b is the device holding cycle b // 64 of the map; among the 4 x 64 sample blocks of one device, at most 8 name blocks of any one owner, and on every device some owner gets exactly 8.
All inputs are finite; a program needn't handle non-finite values.
Results may differ from a plain program's by a relative error of at most 0.0042.
Values may be sent and summed in bfloat16 or wider, within the bound.
No kernel may reach another device: no remote copies, remote signals or barrier semaphores. Data moves between devices by JAX's collectives and lax.ppermute only.
A program may use at most 128 MiB of HBM per device.

v0:
```python
import math

import functools

import jax
import jax.numpy as jnp
from jax import lax
from jax.experimental import pallas as pl
from jax.experimental.pallas import tpu as pltpu
from jax.sharding import PartitionSpec as P

ITERS = 2


highest = lax.Precision.HIGHEST


def phase_pair(first_len, second_len, length, sign):
    first = jnp.arange(first_len, dtype=jnp.int32)[:, None]
    second = jnp.arange(second_len, dtype=jnp.int32)[None, :]
    phases = (first * second % length).astype(jnp.float32) * (sign * 2.0 * math.pi / length)
    return (jnp.cos(phases), jnp.sin(phases))


def forward_cycles(field):
    cycles, length = field.shape
    outer_len = length // 128
    shaped = field.reshape(cycles, outer_len, 128)
    cos_outer, sin_outer = phase_pair(outer_len, outer_len, outer_len, -1.0)
    part_re = jnp.einsum("mj,rjk->rmk", cos_outer, shaped, precision=highest)
    part_im = jnp.einsum("mj,rjk->rmk", sin_outer, shaped, precision=highest)
    cos_twist, sin_twist = phase_pair(outer_len, 128, length, -1.0)
    twist_re = part_re * cos_twist - part_im * sin_twist
    twist_im = part_re * sin_twist + part_im * cos_twist
    cos_inner, sin_inner = phase_pair(128, 128, 128, -1.0)
    spec_re = jnp.einsum("rmk,kn->rmn", twist_re, cos_inner, precision=highest) - jnp.einsum(
        "rmk,kn->rmn", twist_im, sin_inner, precision=highest
    )
    spec_im = jnp.einsum("rmk,kn->rmn", twist_re, sin_inner, precision=highest) + jnp.einsum(
        "rmk,kn->rmn", twist_im, cos_inner, precision=highest
    )
    return (spec_re.reshape(cycles, length), spec_im.reshape(cycles, length))


def inverse_cycles(spec_re, spec_im):
    cycles, length = spec_re.shape
    outer_len = length // 128
    shaped_re = spec_re.reshape(cycles, outer_len, 128)
    shaped_im = spec_im.reshape(cycles, outer_len, 128)
    cos_inner, sin_inner = phase_pair(128, 128, 128, 1.0)
    inner_re = jnp.einsum("rmn,nk->rmk", shaped_re, cos_inner, precision=highest) - jnp.einsum(
        "rmn,nk->rmk", shaped_im, sin_inner, precision=highest
    )
    inner_im = jnp.einsum("rmn,nk->rmk", shaped_re, sin_inner, precision=highest) + jnp.einsum(
        "rmn,nk->rmk", shaped_im, cos_inner, precision=highest
    )
    cos_twist, sin_twist = phase_pair(outer_len, 128, length, 1.0)
    twist_re = inner_re * cos_twist - inner_im * sin_twist
    twist_im = inner_re * sin_twist + inner_im * cos_twist
    cos_outer, sin_outer = phase_pair(outer_len, outer_len, outer_len, 1.0)
    field = jnp.einsum("jm,rmk->rjk", cos_outer, twist_re, precision=highest) - jnp.einsum(
        "jm,rmk->rjk", sin_outer, twist_im, precision=highest
    )
    return field.reshape(cycles, length)


def legendre_filter(owned, legendre, prior_gain, m_own):
    count_here, degrees, total_cycles = legendre.shape
    block_rows = min(512, degrees)

    def one_block(index, running):
        start = index * block_rows
        table = lax.dynamic_slice_in_dim(legendre, start, block_rows, 1)
        analysed = jnp.einsum("mlr,cmr->cml", table, owned, preferred_element_type=jnp.float32)
        degree = start + jnp.arange(block_rows, dtype=jnp.int32)
        keep_rows = degree[None, :] >= m_own[:, None]
        gain_block = lax.dynamic_slice_in_dim(prior_gain, start, block_rows)
        scaled = jnp.where(keep_rows[None], analysed * gain_block, 0.0).astype(jnp.bfloat16)
        return running + jnp.einsum(
            "mlr,cml->cmr", table, scaled, preferred_element_type=jnp.float32
        )

    first_block = 0
    initial = jnp.zeros(owned.shape, jnp.float32)
    summed = lax.fori_loop(first_block, degrees // block_rows, one_block, initial)
    return summed * math.sqrt(total_cycles / degrees)


ROWS = 16


def legendre_body(m_ref, coef_ref, gain_ref, tab_ref, out_ref, *, scale):
    k = pl.program_id(0)
    tab = tab_ref[0]
    coef = coef_ref[0]
    analysed = lax.dot_general(
        coef, tab, (((1,), (1,)), ((), ())), preferred_element_type=jnp.float32
    )
    degree = lax.broadcasted_iota(jnp.int32, analysed.shape, 1)
    keep = degree >= m_ref[k]
    scaled = jnp.where(keep, analysed * gain_ref[...], 0.0).astype(jnp.bfloat16)
    synth = jnp.dot(scaled, tab, preferred_element_type=jnp.float32)
    out_ref[0] = synth * scale


def legendre_pallas(owned, legendre, prior_gain, m_own):
    count_here, degrees, total_cycles = legendre.shape
    coef = jnp.zeros((count_here, ROWS, total_cycles), jnp.bfloat16)
    coef = coef.at[:, :2, :].set(owned.transpose(1, 0, 2))
    gain = prior_gain.reshape(1, degrees)
    grid_spec = pltpu.PrefetchScalarGridSpec(
        num_scalar_prefetch=1,
        grid=(count_here,),
        in_specs=[
            pl.BlockSpec((1, ROWS, total_cycles), lambda k, m: (k, 0, 0)),
            pl.BlockSpec((1, degrees), lambda k, m: (0, 0)),
            pl.BlockSpec((1, degrees, total_cycles), lambda k, m: (k, 0, 0)),
        ],
        out_specs=pl.BlockSpec((1, ROWS, total_cycles), lambda k, m: (k, 0, 0)),
    )
    out = pl.pallas_call(
        functools.partial(legendre_body, scale=math.sqrt(total_cycles / degrees)),
        grid_spec=grid_spec,
        out_shape=jax.ShapeDtypeStruct((count_here, ROWS, total_cycles), jnp.float32),
    )(m_own, coef, gain, legendre)
    return out[:, :2, :].transpose(1, 0, 2)


def pointing_body(w_ref, p_ref, x_ref, s_ref, out_ref, *, tblk, nsamp):
    d = pl.program_id(0)
    point = p_ref[0].reshape(tblk * nsamp, p_ref.shape[3])
    picked = x_ref[0]
    every = lax.dot_general(
        picked, point, (((1,), (1,)), ((), ())), preferred_element_type=jnp.float32
    )
    row = lax.broadcasted_iota(jnp.int32, every.shape, 0)
    col = lax.broadcasted_iota(jnp.int32, every.shape, 1)
    mine = row == col // nsamp
    predicted = jnp.sum(jnp.where(mine, every, 0.0), axis=0, keepdims=True)
    resid = (w_ref[d] * (s_ref[0] - predicted)).astype(jnp.bfloat16)
    spread = jnp.where(mine, jnp.broadcast_to(resid, every.shape), jnp.zeros_like(resid))
    out_ref[0] = jnp.dot(spread, point, preferred_element_type=jnp.float32)


def pointing_pallas(pointing, picked, samples, det_weight):
    dets, times, nsamp, npix = pointing.shape
    tblk = times
    samples_row = samples.reshape(dets, 1, times * nsamp)
    grid_spec = pltpu.PrefetchScalarGridSpec(
        num_scalar_prefetch=1,
        grid=(dets, times // tblk),
        in_specs=[
            pl.BlockSpec((1, tblk, nsamp, npix), lambda d, t, w: (d, t, 0, 0)),
            pl.BlockSpec((1, tblk, npix), lambda d, t, w: (d, t, 0)),
            pl.BlockSpec((1, 1, tblk * nsamp), lambda d, t, w: (d, 0, t)),
        ],
        out_specs=pl.BlockSpec((1, tblk, npix), lambda d, t, w: (d, t, 0)),
    )
    return pl.pallas_call(
        functools.partial(pointing_body, tblk=tblk, nsamp=nsamp),
        grid_spec=grid_spec,
        out_shape=jax.ShapeDtypeStruct((dets, times, npix), jnp.float32),
    )(det_weight, pointing, picked, samples_row)


CAP = 8


STRIDE = 4


def order_pick(m_values):
    count = m_values.shape[0]
    offset = m_values - STRIDE * jnp.arange(count, dtype=jnp.int32)
    return offset[:, None] == jnp.arange(STRIDE, dtype=jnp.int32)[None, :]


def spectrum_out(field, m_values, cycle_offset):
    cycles_here, length = field.shape
    count = m_values.shape[0]
    spec_re, spec_im = forward_cycles(field)
    outer_len = length // 128
    spec_re = spec_re.reshape(cycles_here, outer_len, 128).transpose(0, 2, 1)
    spec_im = spec_im.reshape(cycles_here, outer_len, 128).transpose(0, 2, 1)
    pick = order_pick(m_values)[None]
    band = count * STRIDE
    spec_re = spec_re.reshape(cycles_here, length)[:, :band].reshape(cycles_here, count, STRIDE)
    spec_im = spec_im.reshape(cycles_here, length)[:, :band].reshape(cycles_here, count, STRIDE)
    pick_re = jnp.sum(jnp.where(pick, spec_re, 0.0), axis=2)
    pick_im = jnp.sum(jnp.where(pick, spec_im, 0.0), axis=2)
    phases = (m_values[None, :] * cycle_offset[:, None] % length).astype(jnp.float32) * (
        2.0 * math.pi / length
    )
    cos_phase = jnp.cos(phases)
    sin_phase = jnp.sin(phases)
    norm_factor = 1.0 / math.sqrt(length)
    coef_re = (pick_re * cos_phase + pick_im * sin_phase) * norm_factor
    coef_im = (pick_im * cos_phase - pick_re * sin_phase) * norm_factor
    return coef_re, coef_im, cos_phase, sin_phase


def spectrum_back(back_re, back_im, cos_phase, sin_phase, m_values, length):
    cycles_here = back_re.shape[0]
    count = m_values.shape[0]
    outer_len = length // 128
    mode_weight = jnp.where(m_values == 0, 1.0, 2.0).astype(jnp.float32)[None, :]
    harm_re = mode_weight * (back_re * cos_phase - back_im * sin_phase)
    harm_im = mode_weight * (back_re * sin_phase + back_im * cos_phase)
    pick = order_pick(m_values)[None]
    rest = ((0, 0), (0, length - count * STRIDE))
    full_re = jnp.where(pick, harm_re[:, :, None], 0.0).reshape(cycles_here, count * STRIDE)
    full_im = jnp.where(pick, harm_im[:, :, None], 0.0).reshape(cycles_here, count * STRIDE)
    full_re = jnp.pad(full_re, rest).reshape(cycles_here, 128, outer_len)
    full_im = jnp.pad(full_im, rest).reshape(cycles_here, 128, outer_len)
    full_re = full_re.transpose(0, 2, 1).reshape(cycles_here, length)
    full_im = full_im.transpose(0, 2, 1).reshape(cycles_here, length)
    return inverse_cycles(full_re, full_im) / math.sqrt(2.0 * count)


def on_device(
    samples,
    pointing,
    pix_block,
    det_weight,
    start_map,
    legendre,
    prior_gain,
    m_values,
    cycle_offset,
):
    axes = ("det", "tm")
    cycles_here, length = start_map.shape
    per_cycle = length // 128
    owners = lax.axis_size(axes)
    total_cycles = cycles_here * owners
    blocks_here = cycles_here * per_cycle
    count_here = legendre.shape[0]
    owner_index = lax.axis_index(axes)
    m_own = lax.dynamic_slice_in_dim(m_values, owner_index * count_here, count_here)
    slots = owners * CAP

    flat_pix = pix_block.reshape(-1)
    nloc = flat_pix.shape[0]
    owner_of = flat_pix // blocks_here
    within = flat_pix % blocks_here
    order = jnp.arange(nloc, dtype=jnp.int32)
    same = (owner_of[:, None] == owner_of[None, :]) & (order[None, :] < order[:, None])
    rank = jnp.sum(same.astype(jnp.int32), axis=1)
    slot = owner_of * CAP + rank
    weight_of = jnp.broadcast_to(det_weight[:, None], pix_block.shape).reshape(-1)
    info = jnp.stack([within.astype(jnp.float32), weight_of], axis=1)
    info = jnp.zeros((slots, 2), jnp.float32).at[slot].set(info).reshape(owners, CAP * 2)
    coef_width = 2 * count_here * cycles_here

    def coef_out(field):
        coef_re, coef_im, cos_phase, sin_phase = spectrum_out(field, m_values, cycle_offset)
        outward = jnp.stack([coef_re.T, coef_im.T]).astype(jnp.bfloat16)
        outward = outward.reshape(2, owners, count_here, cycles_here).transpose(1, 0, 2, 3)
        return outward.reshape(owners, coef_width), cos_phase, sin_phase

    def coef_in(part):
        owned = part.reshape(owners, 2, count_here, cycles_here).astype(jnp.bfloat16)
        return owned.transpose(1, 2, 0, 3).reshape(2, count_here, total_cycles)

    first_out, cos_phase, sin_phase = coef_out(start_map)
    info = jnp.concatenate([info, first_out.astype(jnp.float32)], axis=1)
    info_recv = lax.all_to_all(info, axes, 0, 0, tiled=True)
    first_owned = coef_in(info_recv[:, CAP * 2 :])
    info_recv = info_recv[:, : CAP * 2].reshape(slots, 2)
    want = info_recv[:, 0].astype(jnp.int32)
    want_hot = (want[None, :] == jnp.arange(blocks_here, dtype=jnp.int32)[:, None]).astype(jnp.float32)
    hit_weight = jnp.sum(want_hot * info_recv[None, :, 1], axis=1).reshape(cycles_here, per_cycle)
    divisor = jnp.repeat(1.0 + 0.25 * hit_weight, 128, axis=1)
    want_pick = want_hot.T.astype(jnp.bfloat16)

    current = start_map
    for iteration in range(ITERS):
        map_half = current.astype(jnp.bfloat16).reshape(blocks_here, 128)
        rows_out = jnp.dot(want_pick, map_half, preferred_element_type=jnp.float32)
        rows_out = rows_out.astype(jnp.bfloat16).reshape(owners, CAP * 128)
        if iteration == 0:
            rows_in = lax.all_to_all(rows_out, axes, 0, 0, tiled=True).reshape(slots, 128)
            owned = first_owned
        else:
            outward, cos_phase, sin_phase = coef_out(current)
            send_a = jnp.concatenate([rows_out, outward], axis=1)
            recv_a = lax.all_to_all(send_a, axes, 0, 0, tiled=True)
            rows_in = recv_a[:, : CAP * 128].reshape(slots, 128)
            owned = coef_in(recv_a[:, CAP * 128 :])

        picked = rows_in[slot].reshape(pix_block.shape + (128,))
        binned_terms = pointing_pallas(pointing, picked, samples, det_weight)
        binned_send = jnp.zeros((slots, 128), jnp.float32).at[slot].set(binned_terms.reshape(-1, 128))

        synth = legendre_pallas(owned, legendre, prior_gain, m_own)
        synth_send = synth.reshape(2, count_here, owners, cycles_here).transpose(2, 0, 1, 3)
        send_b = jnp.concatenate(
            [binned_send.reshape(owners, CAP * 128), synth_send.reshape(owners, -1)], axis=1
        )
        recv_b = lax.all_to_all(send_b, axes, 0, 0, tiled=True)
        binned_in = recv_b[:, : CAP * 128].reshape(slots, 128)
        binned = jnp.dot(want_hot, binned_in, precision=highest).reshape(cycles_here, length)
        returned = recv_b[:, CAP * 128 :].reshape(owners, 2, count_here, cycles_here)
        returned = returned.transpose(1, 0, 2, 3).reshape(2, owners * count_here, cycles_here)
        filtered = spectrum_back(
            returned[0].T, returned[1].T, cos_phase, sin_phase, m_values, length
        )
        current = current + (binned - filtered) / divisor
    return current


def solution(mesh):
    placed = (
        P("det", "tm", None),
        P("det", "tm", None, None),
        P("det", "tm"),
        P("det"),
        P(("det", "tm"), None),
        P(("det", "tm"), None, None),
        P(),
        P(),
        P(("det", "tm")),
    )
    return jax.shard_map(
        on_device, mesh=mesh, in_specs=placed, out_specs=P(("det", "tm"), None), check_vma=False
    )
```

profile of v0, /device:TPU:1, one launch (start us, length us, event | category | flops | bytes accessed | tf_op | source)
XLA Modules:
  0.0 177.5 jit_solution(17481626984506310808)
XLA Ops:
  1.5 1.0 convolution_bitcast_fusion.2
  2.6 1.1 convolution_bitcast_fusion.3
  8.9 1.3 scatter_custom_fusion
  14.0 11.5 %all-to-all-start = ((f32[128,1,32]{2,1,0:T(1,128)}), f32[128,1,32]{2,1,0:T(1,128)S(1)}, u32[]{:S(2)}, u32[]{:S(2)}) async-start(f32[128,1,32]{2,1,0:T(1,128)} %bitcast.23), calls=%async_computation | async-start | bytes 131072 | tf_op jit(solution)/shard_map/all_to_all | solution.py:267
  26.3 1.3 dynamic_slice.3.m_ref
  27.7 7.6 %all-to-all-done = f32[128,1,32]{2,1,0:T(1,128)S(1)} async-done(((f32[128,1,32]{2,1,0:T(1,128)}), f32[128,1,32]{2,1,0:T(1,128)S(1)}, u32[]{:S(2)}, u32[]{:S(2)}) %all-to-all-start) | async-done | bytes 16416 | tf_op jit(solution)/shard_map/all_to_all | solution.py:267
  36.9 2.2 %reduce.49 = bf16[128,1024]{1,0:T(8,128)(2,1)S(1)} reduce(bf16[128,1,1024]{2,1,0:T(2,128)(2,1)S(1)} %all_to_all.52, bf16[]{:T(256)} %broadcast.1114), dimensions={1}, to_apply=%all_to_all.52.reduce_sub_computation | reduce | bytes 524290 | tf_op jit(solution)/shard_map/all_to_all | solution.py:282
  40.0 4.3 %all-to-all-start.1 = ((bf16[128,2,512]{2,1,0:T(2,128)(2,1)}), bf16[128,2,512]{2,1,0:T(2,128)(2,1)S(1)}, u32[]{:S(2)}, u32[]{:S(2)}) async-start(bf16[128,2,512]{2,1,0:T(2,128)(2,1)} %reshape.1293), calls=%async_computation.1 | async-start | bytes 524288 | tf_op jit(solution)/shard_map/all_to_all | solution.py:282
  44.9 11.0 %shard_map.92 = f32[8,16,128]{2,1,0:T(8,128)} custom-call(s32[8]{0:T(128)} %dynamic_slice.3.m_ref, bf16[8,16,128]{2,1,0:T(8,128)(2,1)} %scatter.33.coef_ref, f32[1,6144]{1,0:T(1,128)} %bitcast.239, bf16[8,6144,128]{2,1,0:T(8,128)(2,1)} %tab_ref.3), custom_call_target="tpu_custom_call" | custom-call | tf_op jit(solution)/shard_map/pallas_call | solution.py:121
  57.1 1.5 reduce.12
  58.7 1.5 gather_fusion
  60.2 8.2 %shard_map.91 = f32[4,64,128]{2,1,0:T(8,128)} custom-call(f32[4]{0:T(128)} %w_ref.3, bf16[4,64,128,128]{3,2,1,0:T(8,128)(2,1)} %p_ref.3, bf16[4,64,128]{2,1,0:T(8,128)(2,1)} %bitcast.230, f32[4,1,8192]{2,1,0:T(1,128)} %bitcast.225), custom_call_target="tpu_custom_call" | custom-call | tf_op jit(solution)/shard_map/pallas_call | solution.py:159
  68.4 1.6 scatter_custom_fusion.1
  70.2 1.4 copy.135
  71.6 9.8 %all-to-all-start.2 = ((f32[128,1,1040]{2,1,0:T(1,128)}), f32[128,1,1040]{2,1,0:T(1,128)S(1)}, u32[]{:S(2)}, u32[]{:S(2)}) async-start(f32[128,1,1040]{2,1,0:T(1,128)} %copy.135), calls=%async_computation.2 | async-start | bytes 1179648 | tf_op jit(solution)/shard_map/all_to_all | solution.py:300
  82.8 13.3 %all-to-all-done.2 = f32[128,1,1040]{2,1,0:T(1,128)S(1)} async-done(((f32[128,1,1040]{2,1,0:T(1,128)}), f32[128,1,1040]{2,1,0:T(1,128)S(1)}, u32[]{:S(2)}, u32[]{:S(2)}) %all-to-all-start.2) | async-done | bytes 532512 | tf_op jit(solution)/shard_map/all_to_all | solution.py:300
  96.1 0.9 copy.136
  110.1 15.9 %all_to_all.58 = bf16[128,2,520]{2,1,0:T(2,128)(2,1)S(1)} all-to-all(bf16[128,2,520]{2,1,0:T(2,128)(2,1)S(1)} %reshape.1295), channel_id=1, replica_groups=mesh['det'=8,'tm'=16] {'det','tm'}, dimensions={0} | all-to-all | bytes 532480 | tf_op jit(solution)/shard_map/all_to_all | solution.py:287
  126.5 0.9 copy.146
  127.7 1.5 gather_fusion.1
  129.8 11.0 %shard_map.94 = f32[8,16,128]{2,1,0:T(8,128)} custom-call(s32[8]{0:T(128)} %dynamic_slice.3.m_ref, bf16[8,16,128]{2,1,0:T(8,128)(2,1)} %scatter.35.coef_ref, f32[1,6144]{1,0:T(1,128)} %bitcast.240, bf16[8,6144,128]{2,1,0:T(8,128)(2,1)} %tab_ref.3), custom_call_target="tpu_custom_call" | custom-call | tf_op jit(solution)/shard_map/pallas_call | solution.py:121
  141.7 8.1 %shard_map.93 = f32[4,64,128]{2,1,0:T(8,128)} custom-call(f32[4]{0:T(128)} %w_ref.3, bf16[4,64,128,128]{3,2,1,0:T(8,128)(2,1)} %p_ref.3, bf16[4,64,128]{2,1,0:T(8,128)(2,1)} %bitcast.229, f32[4,1,8192]{2,1,0:T(1,128)} %bitcast.226), custom_call_target="tpu_custom_call" | custom-call | tf_op jit(solution)/shard_map/pallas_call | solution.py:159
  149.8 1.6 scatter_custom_fusion.2
  152.2 18.5 %all_to_all.59 = f32[128,1,1040]{2,1,0:T(1,128)S(1)} all-to-all(f32[128,1,1040]{2,1,0:T(1,128)S(1)} %copy.151), channel_id=1, replica_groups=mesh['det'=8,'tm'=16] {'det','tm'}, dimensions={0} | all-to-all | bytes 1064960 | tf_op jit(solution)/shard_map/all_to_all | solution.py:300
  (163 shorter events, 38.8 us)
Async XLA Ops:
  14.0 21.3 %all-to-all-start = ((f32[128,1,32]{2,1,0:T(1,128)}), f32[128,1,32]{2,1,0:T(1,128)S(1)}, u32[]{:S(2)}, u32[]{:S(2)}) async-start(f32[128,1,32]{2,1,0:T(1,128)} %bitcast.23), calls=%async_computation | async-start | bytes 131072 | tf_op jit(solution)/shard_map/all_to_all | solution.py:267
  40.0 16.8 %all-to-all-start.1 = ((bf16[128,2,512]{2,1,0:T(2,128)(2,1)}), bf16[128,2,512]{2,1,0:T(2,128)(2,1)S(1)}, u32[]{:S(2)}, u32[]{:S(2)}) async-start(bf16[128,2,512]{2,1,0:T(2,128)(2,1)} %reshape.1293), calls=%async_computation.1 | async-start | bytes 524288 | tf_op jit(solution)/shard_map/all_to_all | solution.py:282
  55.9 41.6 %copy-start = (s32[1024]{0:T(1024)S(1)}, s32[1024]{0:T(1024)}, u32[]{:S(2)}) copy-start(s32[1024]{0:T(1024)} %param.20) | copy-start | bytes 12292
  60.2 42.2 %copy-start.1 = (f32[1,8192]{1,0:T(1,128)S(1)}, f32[1,8192]{1,0:T(1,128)}, u32[]{:S(2)}) copy-start(f32[1,8192]{1,0:T(1,128)} %param.17) | copy-start | bytes 98308
  71.6 24.5 %all-to-all-start.2 = ((f32[128,1,1040]{2,1,0:T(1,128)}), f32[128,1,1040]{2,1,0:T(1,128)S(1)}, u32[]{:S(2)}, u32[]{:S(2)}) async-start(f32[128,1,1040]{2,1,0:T(1,128)} %copy.135), calls=%async_computation.2 | async-start | bytes 1179648 | tf_op jit(solution)/shard_map/all_to_all | solution.py:300
where the time goes:
time: 179 us; the launch traced here: 177 us
  Pallas kernels  38.4 us (21%)
  blocking collectives  34.4 us (19%)
  local copies, waits for them, and re-layouts  32.6 us (18%)
  starting transfers between devices  25.6 us (14%)
  waiting for transfers between devices  20.9 us (12%)
  matrix products  13.7 us (8%)
  other arithmetic  10.4 us (6%)
    pallas_call x2, Pallas kernels, legendre_pallas(): pl.pallas_call(functools.partial(legendre_body, scale=math.sqrt(total_cyc...  22 us
    all_to_all x1, blocking collectives, on_device(): recv_b = lax.all_to_all(send_b, axes, 0, 0, tiled=True)  18.5 us
    pallas_call x2, Pallas kernels, pointing_pallas(): pl.pallas_call(functools.partial(pointing_body, tblk=tblk, nsamp=nsamp),...  16.3 us
    all_to_all x1, blocking collectives, on_device(): recv_a = lax.all_to_all(send_a, axes, 0, 0, tiled=True)  15.9 us
    all_to_all x1, waiting for transfers between devices, on_device(): recv_b = lax.all_to_all(send_b, axes, 0, 0, tiled=True)  13.3 us
    all_to_all x1, starting transfers between devices, on_device(): info_recv = lax.all_to_all(info, axes, 0, 0, tiled=True)  11.5 us
    all_to_all x1, starting transfers between devices, on_device(): recv_b = lax.all_to_all(send_b, axes, 0, 0, tiled=True)  9.79 us
    all_to_all x1, waiting for transfers between devices, on_device(): info_recv = lax.all_to_all(info, axes, 0, 0, tiled=True)  7.58 us
  transfers between devices with their start and end apart: 3, of which 2 were waited for; matrix products, arithmetic and copies ran while one was open for 3% of the time, Pallas kernels for 6%

commit v1 on v0

--- a/solution.py
+++ b/solution.py
@@ -247,6 +247,7 @@
     same = (owner_of[:, None] == owner_of[None, :]) & (order[None, :] < order[:, None])
     rank = jnp.sum(same.astype(jnp.int32), axis=1)
     slot = owner_of * CAP + rank
+    slot_hot = (slot[:, None] == jnp.arange(slots, dtype=jnp.int32)[None, :]).astype(jnp.bfloat16)
     weight_of = jnp.broadcast_to(det_weight[:, None], pix_block.shape).reshape(-1)
     info = jnp.stack([within.astype(jnp.float32), weight_of], axis=1)
     info = jnp.zeros((slots, 2), jnp.float32).at[slot].set(info).reshape(owners, CAP * 2)
@@ -272,6 +273,7 @@
     hit_weight = jnp.sum(want_hot * info_recv[None, :, 1], axis=1).reshape(cycles_here, per_cycle)
     divisor = jnp.repeat(1.0 + 0.25 * hit_weight, 128, axis=1)
     want_pick = want_hot.T.astype(jnp.bfloat16)
+    want_sum = want_hot.astype(jnp.bfloat16)
 
     current = start_map
     for iteration in range(ITERS):
@@ -288,19 +290,28 @@
             rows_in = recv_a[:, : CAP * 128].reshape(slots, 128)
             owned = coef_in(recv_a[:, CAP * 128 :])
 
-        picked = rows_in[slot].reshape(pix_block.shape + (128,))
+        picked = jnp.dot(slot_hot, rows_in, preferred_element_type=jnp.float32)
+        picked = picked.astype(jnp.bfloat16).reshape(pix_block.shape + (128,))
         binned_terms = pointing_pallas(pointing, picked, samples, det_weight)
-        binned_send = jnp.zeros((slots, 128), jnp.float32).at[slot].set(binned_terms.reshape(-1, 128))
+        binned_half = binned_terms.reshape(-1, 128).astype(jnp.bfloat16)
+        binned_send = jnp.dot(slot_hot.T, binned_half, preferred_element_type=jnp.float32)
 
         synth = legendre_pallas(owned, legendre, prior_gain, m_own)
         synth_send = synth.reshape(2, count_here, owners, cycles_here).transpose(2, 0, 1, 3)
+        synth_send = synth_send.reshape(owners, -1)
+        synth_hi = synth_send.astype(jnp.bfloat16)
+        synth_lo = (synth_send - synth_hi.astype(jnp.float32)).astype(jnp.bfloat16)
         send_b = jnp.concatenate(
-            [binned_send.reshape(owners, CAP * 128), synth_send.reshape(owners, -1)], axis=1
+            [binned_send.astype(jnp.bfloat16).reshape(owners, CAP * 128), synth_hi, synth_lo],
+            axis=1,
         )
         recv_b = lax.all_to_all(send_b, axes, 0, 0, tiled=True)
         binned_in = recv_b[:, : CAP * 128].reshape(slots, 128)
-        binned = jnp.dot(want_hot, binned_in, precision=highest).reshape(cycles_here, length)
-        returned = recv_b[:, CAP * 128 :].reshape(owners, 2, count_here, cycles_here)
+        binned = jnp.dot(want_sum, binned_in, preferred_element_type=jnp.float32)
+        binned = binned.reshape(cycles_here, length)
+        returned = recv_b[:, CAP * 128 :].astype(jnp.float32)
+        returned = returned[:, :coef_width] + returned[:, coef_width:]
+        returned = returned.reshape(owners, 2, count_here, cycles_here)
         returned = returned.transpose(1, 0, 2, 3).reshape(2, owners * count_here, cycles_here)
         filtered = spectrum_back(
             returned[0].T, returned[1].T, cos_phase, sin_phase, m_values, length

time: 179 us -> 180 us (level)
  waiting for transfers between devices: 20.9 us -> 29.8 us
  starting transfers between devices: 25.6 us -> 19.8 us
  local copies, waits for them, and re-layouts: 32.6 us -> 27.3 us
  other arithmetic: 10.4 us -> 13.5 us
  matrix products: 13.7 us -> 16.4 us
  blocking collectives: 34.4 us -> 31.8 us
    all_to_all x1, waiting for transfers between devices: 0.01 us -> 11.1 us  [on_device(): lax.all_to_all(rows_out, axes, 0, 0, tiled=True).reshape(slots, 128)]
    all_to_all x1, starting transfers between devices: 9.79 us -> 3.99 us  [on_device(): recv_b = lax.all_to_all(send_b, axes, 0, 0, tiled=True)]
    scatter x2 -> x0, local copies, waits for them, and re-layouts: 3.28 us -> none  [on_device(): jnp.zeros((slots, 128), jnp.float32).at[slot]]
    gather x2 -> x0, local copies, waits for them, and re-layouts: 2.92 us -> none  [on_device(): picked = rows_in[slot].reshape(pix_block.shape + (128,))]
    unnamed x9 -> x15, local copies, waits for them, and re-layouts: 2.21 us -> 5.09 us
    dot_general x2 -> x6, matrix products: 0.68 us -> 3.41 us  [the longest x2 1.95 us: on_device(): picked = jnp.dot(slot_hot, rows_in, preferred_element_type=jnp.float32)]
    all_to_all x1, blocking collectives: 18.5 us -> 15.9 us  [on_device(): recv_b = lax.all_to_all(send_b, axes, 0, 0, tiled=True)]
    all_to_all x4 -> x2, local copies, waits for them, and re-layouts: 3.81 us -> 1.84 us  [on_device(): recv_b = lax.all_to_all(send_b, axes, 0, 0, tiled=True)]
  transfers between devices with their start and end apart: 3 -> 3, of which waited for: 2 -> 3; matrix products, arithmetic and copies ran while one was open for 3% -> 2% of each run, Pallas kernels for 6% -> 0%
where the time goes in v1:
time: 180 us; the launch traced here: 178 us
  Pallas kernels  38.2 us (21%)
  blocking collectives  31.8 us (18%)
  waiting for transfers between devices  29.8 us (17%)
  local copies, waits for them, and re-layouts  27.3 us (15%)
  starting transfers between devices  19.8 us (11%)
  matrix products  16.4 us (9%)
  other arithmetic  13.5 us (8%)
    pallas_call x2, Pallas kernels, legendre_pallas(): pl.pallas_call(functools.partial(legendre_body, scale=math.sqrt(total_cyc...  22 us
    pallas_call x2, Pallas kernels, pointing_pallas(): pl.pallas_call(functools.partial(pointing_body, tblk=tblk, nsamp=nsamp),...  16.2 us
    all_to_all x1, blocking collectives, on_device(): recv_a = lax.all_to_all(send_a, axes, 0, 0, tiled=True)  15.9 us
    all_to_all x1, blocking collectives, on_device(): recv_b = lax.all_to_all(send_b, axes, 0, 0, tiled=True)  15.9 us
    all_to_all x1, waiting for transfers between devices, on_device(): recv_b = lax.all_to_all(send_b, axes, 0, 0, tiled=True)  12 us
    all_to_all x1, starting transfers between devices, on_device(): info_recv = lax.all_to_all(info, axes, 0, 0, tiled=True)  11.5 us
    all_to_all x1, waiting for transfers between devices, on_device(): lax.all_to_all(rows_out, axes, 0, 0, tiled=True).reshape(slots, 128)  11.1 us
    all_to_all x1, waiting for transfers between devices, on_device(): info_recv = lax.all_to_all(info, axes, 0, 0, tiled=True)  6.7 us
  transfers between devices with their start and end apart: 3, of which 3 were waited for; matrix products, arithmetic and copies ran while one was open for 2% of the time, Pallas kernels for 0%

profile of v1, /device:TPU:1, one launch (start us, length us, event | category | flops | bytes accessed | tf_op | source)
XLA Modules:
  0.0 178.4 jit_solution(3247512744211142629)
XLA Ops:
  0.0 1.0 convolution_bitcast_fusion.2
  1.1 1.1 convolution_bitcast_fusion.3
  11.8 1.3 scatter_custom_fusion
  14.0 11.5 %all-to-all-start = ((f32[128,1,32]{2,1,0:T(1,128)}), f32[128,1,32]{2,1,0:T(1,128)S(1)}, u32[]{:S(2)}, u32[]{:S(2)}) async-start(f32[128,1,32]{2,1,0:T(1,128)} %bitcast.23), calls=%async_computation | async-start | bytes 131072 | tf_op jit(solution)/shard_map/all_to_all | solution.py:268
  26.3 1.3 dynamic_slice.3.m_ref
  28.5 6.7 %all-to-all-done = f32[128,1,32]{2,1,0:T(1,128)S(1)} async-done(((f32[128,1,32]{2,1,0:T(1,128)}), f32[128,1,32]{2,1,0:T(1,128)S(1)}, u32[]{:S(2)}, u32[]{:S(2)}) %all-to-all-start) | async-done | bytes 16416 | tf_op jit(solution)/shard_map/all_to_all | solution.py:268
  36.5 11.0 %shard_map.92 = f32[8,16,128]{2,1,0:T(8,128)} custom-call(s32[8]{0:T(128)} %dynamic_slice.3.m_ref, bf16[8,16,128]{2,1,0:T(8,128)(2,1)} %scatter.18.coef_ref, f32[1,6144]{1,0:T(1,128)} %bitcast.246, bf16[8,6144,128]{2,1,0:T(8,128)(2,1)} %tab_ref.3), custom_call_target="tpu_custom_call" | custom-call | tf_op jit(solution)/shard_map/pallas_call | solution.py:121
  49.3 2.1 %reduce.49 = bf16[128,1024]{1,0:T(8,128)(2,1)S(1)} reduce(bf16[128,1,1024]{2,1,0:T(2,128)(2,1)S(1)} %all_to_all.52, bf16[]{:T(256)} %broadcast.1118), dimensions={1}, to_apply=%all_to_all.52.reduce_sub_computation | reduce | bytes 524290 | tf_op jit(solution)/shard_map/all_to_all | solution.py:284
  52.2 4.3 %all-to-all-start.1 = ((bf16[128,2,512]{2,1,0:T(2,128)(2,1)}), bf16[128,2,512]{2,1,0:T(2,128)(2,1)S(1)}, u32[]{:S(2)}, u32[]{:S(2)}) async-start(bf16[128,2,512]{2,1,0:T(2,128)(2,1)} %reshape.1264), calls=%async_computation.1 | async-start | bytes 524288 | tf_op jit(solution)/shard_map/all_to_all | solution.py:284
  56.9 11.1 %all-to-all-done.1 = bf16[128,2,512]{2,1,0:T(2,128)(2,1)S(1)} async-done(((bf16[128,2,512]{2,1,0:T(2,128)(2,1)}), bf16[128,2,512]{2,1,0:T(2,128)(2,1)S(1)}, u32[]{:S(2)}, u32[]{:S(2)}) %all-to-all-start.1) | async-done | bytes 262176 | tf_op jit(solution)/shard_map/all_to_all | solution.py:284
  68.2 1.5 reduce.12
  69.9 1.0 convolution_convert_fusion.5
  70.8 8.1 %shard_map.91 = f32[4,64,128]{2,1,0:T(8,128)} custom-call(f32[4]{0:T(128)} %w_ref.3, bf16[4,64,128,128]{3,2,1,0:T(8,128)(2,1)} %p_ref.3, bf16[4,64,128]{2,1,0:T(8,128)(2,1)} %bitcast.248, f32[4,1,8192]{2,1,0:T(1,128)} %bitcast.236), custom_call_target="tpu_custom_call" | custom-call | tf_op jit(solution)/shard_map/pallas_call | solution.py:159
  78.9 0.9 convert_element_type.268
  81.7 1.1 reshape.1266
  82.7 4.0 %all-to-all-start.2 = ((bf16[128,2,528]{2,1,0:T(2,128)(2,1)}), bf16[128,2,528]{2,1,0:T(2,128)(2,1)S(1)}, u32[]{:S(2)}, u32[]{:S(2)}) async-start(bf16[128,2,528]{2,1,0:T(2,128)(2,1)} %reshape.1266), calls=%async_computation.2 | async-start | bytes 655360 | tf_op jit(solution)/shard_map/all_to_all | solution.py:308
  86.9 12.0 %all-to-all-done.2 = bf16[128,2,528]{2,1,0:T(2,128)(2,1)S(1)} async-done(((bf16[128,2,528]{2,1,0:T(2,128)(2,1)}), bf16[128,2,528]{2,1,0:T(2,128)(2,1)S(1)}, u32[]{:S(2)}, u32[]{:S(2)}) %all-to-all-start.2) | async-done | bytes 270368 | tf_op jit(solution)/shard_map/all_to_all | solution.py:308
  99.4 0.9 copy.137
  113.1 15.9 %all_to_all.58 = bf16[128,2,520]{2,1,0:T(2,128)(2,1)S(1)} all-to-all(bf16[128,2,520]{2,1,0:T(2,128)(2,1)S(1)} %reshape.1268), channel_id=1, replica_groups=mesh['det'=8,'tm'=16] {'det','tm'}, dimensions={0} | all-to-all | bytes 532480 | tf_op jit(solution)/shard_map/all_to_all | solution.py:289
  131.1 11.0 %shard_map.94 = f32[8,16,128]{2,1,0:T(8,128)} custom-call(s32[8]{0:T(128)} %dynamic_slice.3.m_ref, bf16[8,16,128]{2,1,0:T(8,128)(2,1)} %scatter.19.coef_ref, f32[1,6144]{1,0:T(1,128)} %bitcast.247, bf16[8,6144,128]{2,1,0:T(8,128)(2,1)} %tab_ref.3), custom_call_target="tpu_custom_call" | custom-call | tf_op jit(solution)/shard_map/pallas_call | solution.py:121
  143.2 1.0 convolution_convert_fusion.4
  144.1 8.1 %shard_map.93 = f32[4,64,128]{2,1,0:T(8,128)} custom-call(f32[4]{0:T(128)} %w_ref.3, bf16[4,64,128,128]{3,2,1,0:T(8,128)(2,1)} %p_ref.3, bf16[4,64,128]{2,1,0:T(8,128)(2,1)} %bitcast.249, f32[4,1,8192]{2,1,0:T(1,128)} %bitcast.237), custom_call_target="tpu_custom_call" | custom-call | tf_op jit(solution)/shard_map/pallas_call | solution.py:159
  155.4 15.9 %all_to_all.59 = bf16[128,2,528]{2,1,0:T(2,128)(2,1)S(1)} all-to-all(bf16[128,2,528]{2,1,0:T(2,128)(2,1)S(1)} %reshape.1270), channel_id=1, replica_groups=mesh['det'=8,'tm'=16] {'det','tm'}, dimensions={0} | all-to-all | bytes 540672 | tf_op jit(solution)/shard_map/all_to_all | solution.py:308
  171.8 0.9 copy.153
  (175 shorter events, 43.1 us)
Async XLA Ops:
  14.0 21.3 %all-to-all-start = ((f32[128,1,32]{2,1,0:T(1,128)}), f32[128,1,32]{2,1,0:T(1,128)S(1)}, u32[]{:S(2)}, u32[]{:S(2)}) async-start(f32[128,1,32]{2,1,0:T(1,128)} %bitcast.23), calls=%async_computation | async-start | bytes 131072 | tf_op jit(solution)/shard_map/all_to_all | solution.py:268
  47.5 53.3 %copy-start = (s32[1024]{0:T(1024)S(1)}, s32[1024]{0:T(1024)}, u32[]{:S(2)}) copy-start(s32[1024]{0:T(1024)} %param.20) | copy-start | bytes 12292
  52.2 15.8 %all-to-all-start.1 = ((bf16[128,2,512]{2,1,0:T(2,128)(2,1)}), bf16[128,2,512]{2,1,0:T(2,128)(2,1)S(1)}, u32[]{:S(2)}, u32[]{:S(2)}) async-start(bf16[128,2,512]{2,1,0:T(2,128)(2,1)} %reshape.1264), calls=%async_computation.1 | async-start | bytes 524288 | tf_op jit(solution)/shard_map/all_to_all | solution.py:284
  56.5 49.1 %copy-start.1 = (f32[1,8192]{1,0:T(1,128)S(1)}, f32[1,8192]{1,0:T(1,128)}, u32[]{:S(2)}) copy-start(f32[1,8192]{1,0:T(1,128)} %param.17) | copy-start | bytes 98308
  82.7 16.2 %all-to-all-start.2 = ((bf16[128,2,528]{2,1,0:T(2,128)(2,1)}), bf16[128,2,528]{2,1,0:T(2,128)(2,1)S(1)}, u32[]{:S(2)}, u32[]{:S(2)}) async-start(bf16[128,2,528]{2,1,0:T(2,128)(2,1)} %reshape.1266), calls=%async_computation.2 | async-start | bytes 655360 | tf_op jit(solution)/shard_map/all_to_all | solution.py:308

commit v2 on v0

--- a/solution.py
+++ b/solution.py
@@ -61,6 +61,54 @@
     field = jnp.einsum("jm,rmk->rjk", cos_outer, twist_re, precision=highest) - jnp.einsum(
         "jm,rmk->rjk", sin_outer, twist_im, precision=highest
     )
+    return field.reshape(cycles, length)
+
+
+def forward_band(field, band):
+    cycles, length = field.shape
+    outer_len = length // 128
+    band_cols = band // outer_len
+    shaped = field.reshape(cycles, outer_len, 128)
+    cos_outer, sin_outer = phase_pair(outer_len, outer_len, outer_len, -1.0)
+    part = jnp.einsum(
+        "mj,rjk->rmk", jnp.concatenate([cos_outer, sin_outer], axis=0), shaped, precision=highest
+    )
+    part_re, part_im = part[:, :outer_len], part[:, outer_len:]
+    cos_twist, sin_twist = phase_pair(outer_len, 128, length, -1.0)
+    twist = jnp.concatenate(
+        [part_re * cos_twist - part_im * sin_twist, part_re * sin_twist + part_im * cos_twist],
+        axis=2,
+    )
+    cos_inner, sin_inner = phase_pair(128, band_cols, 128, -1.0)
+    inner = jnp.concatenate(
+        [jnp.concatenate([cos_inner, sin_inner], axis=1),
+         jnp.concatenate([-sin_inner, cos_inner], axis=1)],
+        axis=0,
+    )
+    spec = jnp.einsum("rmk,kn->rmn", twist, inner, precision=highest)
+    return spec[:, :, :band_cols], spec[:, :, band_cols:]
+
+
+def inverse_band(spec_re, spec_im, length):
+    cycles, outer_len, band_cols = spec_re.shape
+    cos_inner, sin_inner = phase_pair(band_cols, 128, 128, 1.0)
+    inner = jnp.concatenate(
+        [jnp.concatenate([cos_inner, sin_inner], axis=1),
+         jnp.concatenate([-sin_inner, cos_inner], axis=1)],
+        axis=0,
+    )
+    inner_out = jnp.einsum(
+        "rmn,nk->rmk", jnp.concatenate([spec_re, spec_im], axis=2), inner, precision=highest
+    )
+    inner_re, inner_im = inner_out[:, :, :128], inner_out[:, :, 128:]
+    cos_twist, sin_twist = phase_pair(outer_len, 128, length, 1.0)
+    twist = jnp.concatenate(
+        [inner_re * cos_twist - inner_im * sin_twist, inner_re * sin_twist + inner_im * cos_twist],
+        axis=1,
+    )
+    cos_outer, sin_outer = phase_pair(outer_len, outer_len, outer_len, 1.0)
+    outer = jnp.concatenate([cos_outer, -sin_outer], axis=1)
+    field = jnp.einsum("jm,rmk->rjk", outer, twist, precision=highest)
     return field.reshape(cycles, length)
 
 
@@ -178,14 +226,11 @@
 def spectrum_out(field, m_values, cycle_offset):
     cycles_here, length = field.shape
     count = m_values.shape[0]
-    spec_re, spec_im = forward_cycles(field)
-    outer_len = length // 128
-    spec_re = spec_re.reshape(cycles_here, outer_len, 128).transpose(0, 2, 1)
-    spec_im = spec_im.reshape(cycles_here, outer_len, 128).transpose(0, 2, 1)
+    band = count * STRIDE
+    spec_re, spec_im = forward_band(field, band)
+    spec_re = spec_re.transpose(0, 2, 1).reshape(cycles_here, count, STRIDE)
+    spec_im = spec_im.transpose(0, 2, 1).reshape(cycles_here, count, STRIDE)
     pick = order_pick(m_values)[None]
-    band = count * STRIDE
-    spec_re = spec_re.reshape(cycles_here, length)[:, :band].reshape(cycles_here, count, STRIDE)
-    spec_im = spec_im.reshape(cycles_here, length)[:, :band].reshape(cycles_here, count, STRIDE)
     pick_re = jnp.sum(jnp.where(pick, spec_re, 0.0), axis=2)
     pick_im = jnp.sum(jnp.where(pick, spec_im, 0.0), axis=2)
     phases = (m_values[None, :] * cycle_offset[:, None] % length).astype(jnp.float32) * (
@@ -207,14 +252,12 @@
     harm_re = mode_weight * (back_re * cos_phase - back_im * sin_phase)
     harm_im = mode_weight * (back_re * sin_phase + back_im * cos_phase)
     pick = order_pick(m_values)[None]
-    rest = ((0, 0), (0, length - count * STRIDE))
-    full_re = jnp.where(pick, harm_re[:, :, None], 0.0).reshape(cycles_here, count * STRIDE)
-    full_im = jnp.where(pick, harm_im[:, :, None], 0.0).reshape(cycles_here, count * STRIDE)
-    full_re = jnp.pad(full_re, rest).reshape(cycles_here, 128, outer_len)
-    full_im = jnp.pad(full_im, rest).reshape(cycles_here, 128, outer_len)
-    full_re = full_re.transpose(0, 2, 1).reshape(cycles_here, length)
-    full_im = full_im.transpose(0, 2, 1).reshape(cycles_here, length)
-    return inverse_cycles(full_re, full_im) / math.sqrt(2.0 * count)
+    band_cols = count * STRIDE // outer_len
+    full_re = jnp.where(pick, harm_re[:, :, None], 0.0).reshape(cycles_here, band_cols, outer_len)
+    full_im = jnp.where(pick, harm_im[:, :, None], 0.0).reshape(cycles_here, band_cols, outer_len)
+    full_re = full_re.transpose(0, 2, 1)
+    full_im = full_im.transpose(0, 2, 1)
+    return inverse_band(full_re, full_im, length) / math.sqrt(2.0 * count)
 
 
 def on_device(

time: 179 us -> 168 us (0.939)
  matrix products: 13.7 us -> 4.12 us
  local copies, waits for them, and re-layouts: 32.6 us -> 30.4 us
    dot_general x24 -> x8, matrix products: 12.4 us -> 2.79 us  [the longest x2 1.15 us: forward_band(): jnp.einsum('mj,rjk->rmk', jnp.concatenate([cos_outer, sin_outer], axis=0)...]
  transfers between devices with their start and end apart: 3 -> 3, of which waited for: 2 -> 2; matrix products, arithmetic and copies ran while one was open for 3% -> 3% of each run, Pallas kernels for 6% -> 7%
where the time goes in v2:
time: 168 us; the launch traced here: 167 us
  Pallas kernels  38.2 us (23%)
  blocking collectives  34.4 us (20%)
  local copies, waits for them, and re-layouts  30.4 us (18%)
  starting transfers between devices  25.6 us (15%)
  waiting for transfers between devices  20.8 us (12%)
  other arithmetic  12.1 us (7%)
  matrix products  4.12 us (2%)
    pallas_call x2, Pallas kernels, legendre_pallas(): pl.pallas_call(functools.partial(legendre_body, scale=math.sqrt(total_cyc...  22 us
    all_to_all x1, blocking collectives, on_device(): recv_b = lax.all_to_all(send_b, axes, 0, 0, tiled=True)  18.5 us
    pallas_call x2, Pallas kernels, pointing_pallas(): pl.pallas_call(functools.partial(pointing_body, tblk=tblk, nsamp=nsamp),...  16.2 us
    all_to_all x1, blocking collectives, on_device(): recv_a = lax.all_to_all(send_a, axes, 0, 0, tiled=True)  15.9 us
    all_to_all x1, waiting for transfers between devices, on_device(): recv_b = lax.all_to_all(send_b, axes, 0, 0, tiled=True)  13.5 us
    all_to_all x1, starting transfers between devices, on_device(): info_recv = lax.all_to_all(info, axes, 0, 0, tiled=True)  11.5 us
    all_to_all x1, starting transfers between devices, on_device(): recv_b = lax.all_to_all(send_b, axes, 0, 0, tiled=True)  9.78 us
    all_to_all x1, waiting for transfers between devices, on_device(): info_recv = lax.all_to_all(info, axes, 0, 0, tiled=True)  7.27 us
  transfers between devices with their start and end apart: 3, of which 2 were waited for; matrix products, arithmetic and copies ran while one was open for 3% of the time, Pallas kernels for 7%

profile of v2, /device:TPU:1, one launch (start us, length us, event | category | flops | bytes accessed | tf_op | source)
XLA Modules:
  0.0 166.9 jit_solution(8769766104024910217)
XLA Ops:
  4.6 0.9 convolution_bitcast_fusion.3
  6.4 1.3 scatter_custom_fusion
  10.9 11.5 %all-to-all-start = ((f32[128,1,32]{2,1,0:T(1,128)}), f32[128,1,32]{2,1,0:T(1,128)S(1)}, u32[]{:S(2)}, u32[]{:S(2)}) async-start(f32[128,1,32]{2,1,0:T(1,128)} %bitcast.16), calls=%async_computation | async-start | bytes 131072 | tf_op jit(solution)/shard_map/all_to_all | solution.py:310
  23.6 1.3 dynamic_slice.3.m_ref
  25.0 7.3 %all-to-all-done = f32[128,1,32]{2,1,0:T(1,128)S(1)} async-done(((f32[128,1,32]{2,1,0:T(1,128)}), f32[128,1,32]{2,1,0:T(1,128)S(1)}, u32[]{:S(2)}, u32[]{:S(2)}) %all-to-all-start) | async-done | bytes 16416 | tf_op jit(solution)/shard_map/all_to_all | solution.py:310
  33.9 2.2 %reduce.17 = bf16[128,1024]{1,0:T(8,128)(2,1)S(1)} reduce(bf16[128,1,1024]{2,1,0:T(2,128)(2,1)S(1)} %all_to_all.52, bf16[]{:T(256)} %broadcast.972), dimensions={1}, to_apply=%all_to_all.52.reduce_sub_computation | reduce | bytes 524290 | tf_op jit(solution)/shard_map/all_to_all | solution.py:325
  37.0 4.3 %all-to-all-start.1 = ((bf16[128,2,512]{2,1,0:T(2,128)(2,1)}), bf16[128,2,512]{2,1,0:T(2,128)(2,1)S(1)}, u32[]{:S(2)}, u32[]{:S(2)}) async-start(bf16[128,2,512]{2,1,0:T(2,128)(2,1)} %reshape.1249), calls=%async_computation.1 | async-start | bytes 524288 | tf_op jit(solution)/shard_map/all_to_all | solution.py:325
  41.9 11.0 %shard_map.92 = f32[8,16,128]{2,1,0:T(8,128)} custom-call(s32[8]{0:T(128)} %dynamic_slice.3.m_ref, bf16[8,16,128]{2,1,0:T(8,128)(2,1)} %scatter.33.coef_ref, f32[1,6144]{1,0:T(1,128)} %bitcast.205, bf16[8,6144,128]{2,1,0:T(8,128)(2,1)} %tab_ref.3), custom_call_target="tpu_custom_call" | custom-call | tf_op jit(solution)/shard_map/pallas_call | solution.py:169
  54.1 1.5 reduce.10
  55.7 1.5 gather_fusion
  57.2 8.1 %shard_map.91 = f32[4,64,128]{2,1,0:T(8,128)} custom-call(f32[4]{0:T(128)} %w_ref.3, bf16[4,64,128,128]{3,2,1,0:T(8,128)(2,1)} %p_ref.3, bf16[4,64,128]{2,1,0:T(8,128)(2,1)} %bitcast.198, f32[4,1,8192]{2,1,0:T(1,128)} %bitcast.191), custom_call_target="tpu_custom_call" | custom-call | tf_op jit(solution)/shard_map/pallas_call | solution.py:207
  65.3 1.8 %scatter_custom_fusion.1 = f32[1024,128]{1,0:T(8,128)S(1)} fusion(s32[256]{0:T(256)S(1)} %bitcast.215, f32[256,128]{1,0:T(8,128)} %bitcast.200, f32[]{:T(128)} %constant.173.clone.1), kind=kCustom, calls=%fused_computation.33 | custom fusion | bytes 524800 | tf_op jit(solution)/shard_map/scatter | solution.py:336
  67.2 1.4 copy.135
  68.7 9.8 %all-to-all-start.2 = ((f32[128,1,1040]{2,1,0:T(1,128)}), f32[128,1,1040]{2,1,0:T(1,128)S(1)}, u32[]{:S(2)}, u32[]{:S(2)}) async-start(f32[128,1,1040]{2,1,0:T(1,128)} %copy.135), calls=%async_computation.2 | async-start | bytes 1179648 | tf_op jit(solution)/shard_map/all_to_all | solution.py:343
  79.7 13.5 %all-to-all-done.2 = f32[128,1,1040]{2,1,0:T(1,128)S(1)} async-done(((f32[128,1,1040]{2,1,0:T(1,128)}), f32[128,1,1040]{2,1,0:T(1,128)S(1)}, u32[]{:S(2)}, u32[]{:S(2)}) %all-to-all-start.2) | async-done | bytes 532512 | tf_op jit(solution)/shard_map/all_to_all | solution.py:343
  93.2 0.9 copy.136
  101.7 15.9 %all_to_all.58 = bf16[128,2,520]{2,1,0:T(2,128)(2,1)S(1)} all-to-all(bf16[128,2,520]{2,1,0:T(2,128)(2,1)S(1)} %reshape.1251), channel_id=1, replica_groups=mesh['det'=8,'tm'=16] {'det','tm'}, dimensions={0} | all-to-all | bytes 532480 | tf_op jit(solution)/shard_map/all_to_all | solution.py:330
  118.1 0.9 copy.146
  119.3 1.5 gather_fusion.1
  121.4 11.0 %shard_map.94 = f32[8,16,128]{2,1,0:T(8,128)} custom-call(s32[8]{0:T(128)} %dynamic_slice.3.m_ref, bf16[8,16,128]{2,1,0:T(8,128)(2,1)} %scatter.35.coef_ref, f32[1,6144]{1,0:T(1,128)} %bitcast.206, bf16[8,6144,128]{2,1,0:T(8,128)(2,1)} %tab_ref.3), custom_call_target="tpu_custom_call" | custom-call | tf_op jit(solution)/shard_map/pallas_call | solution.py:169
  133.3 8.1 %shard_map.93 = f32[4,64,128]{2,1,0:T(8,128)} custom-call(f32[4]{0:T(128)} %w_ref.3, bf16[4,64,128,128]{3,2,1,0:T(8,128)(2,1)} %p_ref.3, bf16[4,64,128]{2,1,0:T(8,128)(2,1)} %bitcast.197, f32[4,1,8192]{2,1,0:T(1,128)} %bitcast.192), custom_call_target="tpu_custom_call" | custom-call | tf_op jit(solution)/shard_map/pallas_call | solution.py:207
  141.4 1.9 %scatter_custom_fusion.2 = f32[1024,128]{1,0:T(8,128)S(1)} fusion(s32[256]{0:T(256)S(1)} %bitcast.216, f32[256,128]{1,0:T(8,128)} %bitcast.199, f32[]{:T(128)} %constant.173.clone.1), kind=kCustom, calls=%fused_computation.31 | custom fusion | bytes 524800 | tf_op jit(solution)/shard_map/scatter | solution.py:336
  144.0 18.5 %all_to_all.59 = f32[128,1,1040]{2,1,0:T(1,128)S(1)} all-to-all(f32[128,1,1040]{2,1,0:T(1,128)S(1)} %copy.151), channel_id=1, replica_groups=mesh['det'=8,'tm'=16] {'det','tm'}, dimensions={0} | all-to-all | bytes 1064960 | tf_op jit(solution)/shard_map/all_to_all | solution.py:343
  162.6 0.9 copy.152
  (144 shorter events, 28.5 us)
Async XLA Ops:
  10.9 21.3 %all-to-all-start = ((f32[128,1,32]{2,1,0:T(1,128)}), f32[128,1,32]{2,1,0:T(1,128)S(1)}, u32[]{:S(2)}, u32[]{:S(2)}) async-start(f32[128,1,32]{2,1,0:T(1,128)} %bitcast.16), calls=%async_computation | async-start | bytes 131072 | tf_op jit(solution)/shard_map/all_to_all | solution.py:310
  37.0 16.8 %all-to-all-start.1 = ((bf16[128,2,512]{2,1,0:T(2,128)(2,1)}), bf16[128,2,512]{2,1,0:T(2,128)(2,1)S(1)}, u32[]{:S(2)}, u32[]{:S(2)}) async-start(bf16[128,2,512]{2,1,0:T(2,128)(2,1)} %reshape.1249), calls=%async_computation.1 | async-start | bytes 524288 | tf_op jit(solution)/shard_map/all_to_all | solution.py:325
  52.9 42.3 %copy-start.1 = (s32[1024]{0:T(1024)S(1)}, s32[1024]{0:T(1024)}, u32[]{:S(2)}) copy-start(s32[1024]{0:T(1024)} %param.20) | copy-start | bytes 12292
  54.0 43.0 %copy-start = (f32[1,8192]{1,0:T(1,128)S(1)}, f32[1,8192]{1,0:T(1,128)}, u32[]{:S(2)}) copy-start(f32[1,8192]{1,0:T(1,128)} %param.17) | copy-start | bytes 98308
  68.7 24.5 %all-to-all-start.2 = ((f32[128,1,1040]{2,1,0:T(1,128)}), f32[128,1,1040]{2,1,0:T(1,128)S(1)}, u32[]{:S(2)}, u32[]{:S(2)}) async-start(f32[128,1,1040]{2,1,0:T(1,128)} %copy.135), calls=%async_computation.2 | async-start | bytes 1179648 | tf_op jit(solution)/shard_map/all_to_all | solution.py:343

commit v3 on v2

--- a/solution.py
+++ b/solution.py
@@ -137,7 +137,7 @@
 ROWS = 16
 
 
-def legendre_body(m_ref, coef_ref, gain_ref, tab_ref, out_ref, *, scale):
+def legendre_body(base_ref, m_ref, coef_ref, gain_ref, tab_ref, out_ref, *, scale):
     k = pl.program_id(0)
     tab = tab_ref[0]
     coef = coef_ref[0]
@@ -145,32 +145,32 @@
         coef, tab, (((1,), (1,)), ((), ())), preferred_element_type=jnp.float32
     )
     degree = lax.broadcasted_iota(jnp.int32, analysed.shape, 1)
-    keep = degree >= m_ref[k]
+    keep = degree >= m_ref[base_ref[0] + k]
     scaled = jnp.where(keep, analysed * gain_ref[...], 0.0).astype(jnp.bfloat16)
     synth = jnp.dot(scaled, tab, preferred_element_type=jnp.float32)
     out_ref[0] = synth * scale
 
 
-def legendre_pallas(owned, legendre, prior_gain, m_own):
+def legendre_pallas(owned, legendre, prior_gain, m_values, first):
     count_here, degrees, total_cycles = legendre.shape
     coef = jnp.zeros((count_here, ROWS, total_cycles), jnp.bfloat16)
     coef = coef.at[:, :2, :].set(owned.transpose(1, 0, 2))
     gain = prior_gain.reshape(1, degrees)
     grid_spec = pltpu.PrefetchScalarGridSpec(
-        num_scalar_prefetch=1,
+        num_scalar_prefetch=2,
         grid=(count_here,),
         in_specs=[
-            pl.BlockSpec((1, ROWS, total_cycles), lambda k, m: (k, 0, 0)),
-            pl.BlockSpec((1, degrees), lambda k, m: (0, 0)),
-            pl.BlockSpec((1, degrees, total_cycles), lambda k, m: (k, 0, 0)),
+            pl.BlockSpec((1, ROWS, total_cycles), lambda k, b, m: (k, 0, 0)),
+            pl.BlockSpec((1, degrees), lambda k, b, m: (0, 0)),
+            pl.BlockSpec((1, degrees, total_cycles), lambda k, b, m: (k, 0, 0)),
         ],
-        out_specs=pl.BlockSpec((1, ROWS, total_cycles), lambda k, m: (k, 0, 0)),
+        out_specs=pl.BlockSpec((1, ROWS, total_cycles), lambda k, b, m: (k, 0, 0)),
     )
     out = pl.pallas_call(
         functools.partial(legendre_body, scale=math.sqrt(total_cycles / degrees)),
         grid_spec=grid_spec,
         out_shape=jax.ShapeDtypeStruct((count_here, ROWS, total_cycles), jnp.float32),
-    )(m_own, coef, gain, legendre)
+    )(first, m_values, coef, gain, legendre)
     return out[:, :2, :].transpose(1, 0, 2)
 
 
@@ -279,7 +279,7 @@
     blocks_here = cycles_here * per_cycle
     count_here = legendre.shape[0]
     owner_index = lax.axis_index(axes)
-    m_own = lax.dynamic_slice_in_dim(m_values, owner_index * count_here, count_here)
+    first_order = jnp.full((1,), owner_index * count_here, jnp.int32)
     slots = owners * CAP
 
     flat_pix = pix_block.reshape(-1)
@@ -290,6 +290,7 @@
     same = (owner_of[:, None] == owner_of[None, :]) & (order[None, :] < order[:, None])
     rank = jnp.sum(same.astype(jnp.int32), axis=1)
     slot = owner_of * CAP + rank
+    slot_hot = slot[:, None] == jnp.arange(slots, dtype=jnp.int32)[None, :]
     weight_of = jnp.broadcast_to(det_weight[:, None], pix_block.shape).reshape(-1)
     info = jnp.stack([within.astype(jnp.float32), weight_of], axis=1)
     info = jnp.zeros((slots, 2), jnp.float32).at[slot].set(info).reshape(owners, CAP * 2)
@@ -331,11 +332,14 @@
             rows_in = recv_a[:, : CAP * 128].reshape(slots, 128)
             owned = coef_in(recv_a[:, CAP * 128 :])
 
-        picked = rows_in[slot].reshape(pix_block.shape + (128,))
+        picked = jnp.dot(slot_hot.astype(jnp.bfloat16), rows_in, preferred_element_type=jnp.float32)
+        picked = picked.astype(jnp.bfloat16).reshape(pix_block.shape + (128,))
         binned_terms = pointing_pallas(pointing, picked, samples, det_weight)
-        binned_send = jnp.zeros((slots, 128), jnp.float32).at[slot].set(binned_terms.reshape(-1, 128))
-
-        synth = legendre_pallas(owned, legendre, prior_gain, m_own)
+        binned_send = jnp.dot(
+            slot_hot.T.astype(jnp.float32), binned_terms.reshape(-1, 128), precision=highest
+        )
+
+        synth = legendre_pallas(owned, legendre, prior_gain, m_values, first_order)
         synth_send = synth.reshape(2, count_here, owners, cycles_here).transpose(2, 0, 1, 3)
         send_b = jnp.concatenate(
             [binned_send.reshape(owners, CAP * 128), synth_send.reshape(owners, -1)], axis=1

time: 168 us -> 168 us (level)
  local copies, waits for them, and re-layouts: 30.4 us -> 23 us
  matrix products: 4.12 us -> 10 us
    dot_general x0 -> x4, matrix products: none -> 5.91 us  [the longest x2 3.96 us: on_device(): jnp.dot(slot_hot.T.astype(jnp.float32), binned_terms.reshape(-1, 128), pr...]
    scatter x2 -> x0, local copies, waits for them, and re-layouts: 3.68 us -> none  [on_device(): jnp.zeros((slots, 128), jnp.float32).at[slot]]
    gather x2 -> x0, local copies, waits for them, and re-layouts: 2.92 us -> none  [on_device(): picked = rows_in[slot].reshape(pix_block.shape + (128,))]
  transfers between devices with their start and end apart: 3 -> 3, of which waited for: 2 -> 2; matrix products, arithmetic and copies ran while one was open for 3% -> 2% of each run, Pallas kernels for 7% -> 7%
where the time goes in v3:
time: 168 us; the launch traced here: 167 us
  Pallas kernels  38.3 us (23%)
  blocking collectives  34.4 us (20%)
  starting transfers between devices  25.6 us (15%)
  local copies, waits for them, and re-layouts  23 us (14%)
  waiting for transfers between devices  22.1 us (13%)
  other arithmetic  12.5 us (7%)
  matrix products  10 us (6%)
    pallas_call x2, Pallas kernels, legendre_pallas(): pl.pallas_call(functools.partial(legendre_body, scale=math.sqrt(total_cyc...  22.1 us
    all_to_all x1, blocking collectives, on_device(): recv_b = lax.all_to_all(send_b, axes, 0, 0, tiled=True)  18.5 us
    pallas_call x2, Pallas kernels, pointing_pallas(): pl.pallas_call(functools.partial(pointing_body, tblk=tblk, nsamp=nsamp),...  16.2 us
    all_to_all x1, blocking collectives, on_device(): recv_a = lax.all_to_all(send_a, axes, 0, 0, tiled=True)  15.9 us
    all_to_all x1, waiting for transfers between devices, on_device(): recv_b = lax.all_to_all(send_b, axes, 0, 0, tiled=True)  13.5 us
    all_to_all x1, starting transfers between devices, on_device(): info_recv = lax.all_to_all(info, axes, 0, 0, tiled=True)  11.5 us
    all_to_all x1, starting transfers between devices, on_device(): recv_b = lax.all_to_all(send_b, axes, 0, 0, tiled=True)  9.78 us
    all_to_all x1, waiting for transfers between devices, on_device(): info_recv = lax.all_to_all(info, axes, 0, 0, tiled=True)  8.61 us
  transfers between devices with their start and end apart: 3, of which 2 were waited for; matrix products, arithmetic and copies ran while one was open for 2% of the time, Pallas kernels for 7%

profile of v3, /device:TPU:1, one launch (start us, length us, event | category | flops | bytes accessed | tf_op | source)
XLA Modules:
  0.0 167.3 jit_solution(10653999561182141440)
XLA Ops:
  4.6 0.9 convolution_bitcast_fusion.3
  6.4 1.3 scatter_custom_fusion
  10.9 11.5 %all-to-all-start = ((f32[128,1,32]{2,1,0:T(1,128)}), f32[128,1,32]{2,1,0:T(1,128)S(1)}, u32[]{:S(2)}, u32[]{:S(2)}) async-start(f32[128,1,32]{2,1,0:T(1,128)} %bitcast.16), calls=%async_computation | async-start | bytes 131072 | tf_op jit(solution)/shard_map/all_to_all | solution.py:311
  23.6 8.6 %all-to-all-done = f32[128,1,32]{2,1,0:T(1,128)S(1)} async-done(((f32[128,1,32]{2,1,0:T(1,128)}), f32[128,1,32]{2,1,0:T(1,128)S(1)}, u32[]{:S(2)}, u32[]{:S(2)}) %all-to-all-start) | async-done | bytes 16416 | tf_op jit(solution)/shard_map/all_to_all | solution.py:311
  33.9 2.4 %reduce.17 = bf16[128,1024]{1,0:T(8,128)(2,1)S(1)} reduce(bf16[128,1,1024]{2,1,0:T(2,128)(2,1)S(1)} %all_to_all.52, bf16[]{:T(256)} %broadcast.976), dimensions={1}, to_apply=%all_to_all.52.reduce_sub_computation | reduce | bytes 524290 | tf_op jit(solution)/shard_map/all_to_all | solution.py:326
  37.1 4.3 %all-to-all-start.1 = ((bf16[128,2,512]{2,1,0:T(2,128)(2,1)}), bf16[128,2,512]{2,1,0:T(2,128)(2,1)S(1)}, u32[]{:S(2)}, u32[]{:S(2)}) async-start(bf16[128,2,512]{2,1,0:T(2,128)(2,1)} %reshape.1224), calls=%async_computation.1 | async-start | bytes 524288 | tf_op jit(solution)/shard_map/all_to_all | solution.py:326
  42.1 11.1 %shard_map.92 = f32[8,16,128]{2,1,0:T(8,128)} custom-call(s32[1]{0:T(128)} %bitcast.21.base_ref, s32[1024]{0:T(1024)} %m_ref.3, bf16[8,16,128]{2,1,0:T(8,128)(2,1)} %scatter.18.coef_ref, f32[1,6144]{1,0:T(1,128)} %bitcast.206, bf16[8,6144,128]{2,1,0:T(8,128)(2,1)} %tab_ref.3), custom_call_target="tpu_custom_call" | custom-call | tf_op jit(solution)/shard_map/pallas_call | solution.py:169
  54.2 1.7 %reduce.10 = bf16[128,1024]{1,0:T(8,128)(2,1)S(1)} reduce(bf16[128,1,1024]{2,1,0:T(2,128)(2,1)S(1)} %reshape.1225, bf16[]{:T(256)} %constant.213), dimensions={1}, to_apply=%all_to_all.42.reduce_sub_computation | reduce | bytes 524290 | tf_op jit(solution)/shard_map/all_to_all | solution.py:326
  56.0 1.0 convolution_convert_fusion.3
  57.0 8.1 %shard_map.91 = f32[4,64,128]{2,1,0:T(8,128)} custom-call(f32[4]{0:T(128)} %w_ref.3, bf16[4,64,128,128]{3,2,1,0:T(8,128)(2,1)} %p_ref.3, bf16[4,64,128]{2,1,0:T(8,128)(2,1)} %bitcast.209, f32[4,1,8192]{2,1,0:T(1,128)} %bitcast.194), custom_call_target="tpu_custom_call" | custom-call | tf_op jit(solution)/shard_map/pallas_call | solution.py:207
  65.1 2.0 %fusion.1 = f32[1024,128]{1,0:T(8,128)S(1)} fusion(f32[256,128]{1,0:T(8,128)} %bitcast.197, s32[256]{0:T(256)S(1)} %multiply_add_fusion.4), kind=kOutput, calls=%fused_computation.15 | convolution fusion | flops 402915328 | bytes 656384 | tf_op jit(solution)/shard_map/dot_general | solution.py:338
  67.4 1.5 copy.134
  68.9 9.8 %all-to-all-start.2 = ((f32[128,1,1040]{2,1,0:T(1,128)}), f32[128,1,1040]{2,1,0:T(1,128)S(1)}, u32[]{:S(2)}, u32[]{:S(2)}) async-start(f32[128,1,1040]{2,1,0:T(1,128)} %copy.134), calls=%async_computation.2 | async-start | bytes 1179648 | tf_op jit(solution)/shard_map/all_to_all | solution.py:347
  79.9 13.5 %all-to-all-done.2 = f32[128,1,1040]{2,1,0:T(1,128)S(1)} async-done(((f32[128,1,1040]{2,1,0:T(1,128)}), f32[128,1,1040]{2,1,0:T(1,128)S(1)}, u32[]{:S(2)}, u32[]{:S(2)}) %all-to-all-start.2) | async-done | bytes 532512 | tf_op jit(solution)/shard_map/all_to_all | solution.py:347
  93.4 0.9 copy.135
  101.9 15.9 %all_to_all.58 = bf16[128,2,520]{2,1,0:T(2,128)(2,1)S(1)} all-to-all(bf16[128,2,520]{2,1,0:T(2,128)(2,1)S(1)} %reshape.1226), channel_id=1, replica_groups=mesh['det'=8,'tm'=16] {'det','tm'}, dimensions={0} | all-to-all | bytes 532480 | tf_op jit(solution)/shard_map/all_to_all | solution.py:331
  118.3 0.9 copy.145
  119.6 1.0 convolution_convert_fusion.2
  121.2 11.1 %shard_map.94 = f32[8,16,128]{2,1,0:T(8,128)} custom-call(s32[1]{0:T(128)} %bitcast.21.base_ref, s32[1024]{0:T(1024)} %m_ref.3, bf16[8,16,128]{2,1,0:T(8,128)(2,1)} %scatter.19.coef_ref, f32[1,6144]{1,0:T(1,128)} %bitcast.207, bf16[8,6144,128]{2,1,0:T(8,128)(2,1)} %tab_ref.3), custom_call_target="tpu_custom_call" | custom-call | tf_op jit(solution)/shard_map/pallas_call | solution.py:169
  133.0 8.1 %shard_map.93 = f32[4,64,128]{2,1,0:T(8,128)} custom-call(f32[4]{0:T(128)} %w_ref.3, bf16[4,64,128,128]{3,2,1,0:T(8,128)(2,1)} %p_ref.3, bf16[4,64,128]{2,1,0:T(8,128)(2,1)} %bitcast.208, f32[4,1,8192]{2,1,0:T(1,128)} %bitcast.195), custom_call_target="tpu_custom_call" | custom-call | tf_op jit(solution)/shard_map/pallas_call | solution.py:207
  141.1 2.0 %fusion = f32[1024,128]{1,0:T(8,128)S(1)} fusion(f32[256,128]{1,0:T(8,128)} %bitcast.196, s32[256]{0:T(256)S(1)} %multiply_add_fusion.4), kind=kOutput, calls=%fused_computation.14 | convolution fusion | flops 402915328 | bytes 656384 | tf_op jit(solution)/shard_map/dot_general | solution.py:338
  143.5 0.9 copy.150
  144.4 18.5 %all_to_all.59 = f32[128,1,1040]{2,1,0:T(1,128)S(1)} all-to-all(f32[128,1,1040]{2,1,0:T(1,128)S(1)} %copy.150), channel_id=1, replica_groups=mesh['det'=8,'tm'=16] {'det','tm'}, dimensions={0} | all-to-all | bytes 1064960 | tf_op jit(solution)/shard_map/all_to_all | solution.py:347
  162.9 0.9 copy.151
  (145 shorter events, 28.1 us)
Async XLA Ops:
  10.9 21.3 %all-to-all-start = ((f32[128,1,32]{2,1,0:T(1,128)}), f32[128,1,32]{2,1,0:T(1,128)S(1)}, u32[]{:S(2)}, u32[]{:S(2)}) async-start(f32[128,1,32]{2,1,0:T(1,128)} %bitcast.16), calls=%async_computation | async-start | bytes 131072 | tf_op jit(solution)/shard_map/all_to_all | solution.py:311
  37.1 16.8 %all-to-all-start.1 = ((bf16[128,2,512]{2,1,0:T(2,128)(2,1)}), bf16[128,2,512]{2,1,0:T(2,128)(2,1)S(1)}, u32[]{:S(2)}, u32[]{:S(2)}) async-start(bf16[128,2,512]{2,1,0:T(2,128)(2,1)} %reshape.1224), calls=%async_computation.1 | async-start | bytes 524288 | tf_op jit(solution)/shard_map/all_to_all | solution.py:326
  53.2 42.3 %copy-start.1 = (s32[1024]{0:T(1024)S(1)}, s32[1024]{0:T(1024)}, u32[]{:S(2)}) copy-start(s32[1024]{0:T(1024)} %m_ref.3) | copy-start | bytes 12292
  56.0 41.2 %copy-start = (f32[1,8192]{1,0:T(1,128)S(1)}, f32[1,8192]{1,0:T(1,128)}, u32[]{:S(2)}) copy-start(f32[1,8192]{1,0:T(1,128)} %param.17) | copy-start | bytes 98308
  68.9 24.5 %all-to-all-start.2 = ((f32[128,1,1040]{2,1,0:T(1,128)}), f32[128,1,1040]{2,1,0:T(1,128)S(1)}, u32[]{:S(2)}, u32[]{:S(2)}) async-start(f32[128,1,1040]{2,1,0:T(1,128)} %copy.134), calls=%async_computation.2 | async-start | bytes 1179648 | tf_op jit(solution)/shard_map/all_to_all | solution.py:347
  132.3 32.7 %copy-start.2 = (s32[1024]{0:T(1024)S(1)}, s32[1024]{0:T(1024)}, u32[]{:S(2)}) copy-start(s32[1024]{0:T(1024)} %m_ref.3) | copy-start | bytes 12292

commit v4 on v3

--- a/solution.py
+++ b/solution.py
@@ -323,12 +323,15 @@
         rows_out = jnp.dot(want_pick, map_half, preferred_element_type=jnp.float32)
         rows_out = rows_out.astype(jnp.bfloat16).reshape(owners, CAP * 128)
         if iteration == 0:
-            rows_in = lax.all_to_all(rows_out, axes, 0, 0, tiled=True).reshape(slots, 128)
+            rows_in = lax.all_to_all(rows_out.reshape(owners, 1, -1), axes, 0, 0, tiled=True)
+            rows_in = rows_in.reshape(slots, 128)
             owned = first_owned
         else:
             outward, cos_phase, sin_phase = coef_out(current)
-            send_a = jnp.concatenate([rows_out, outward], axis=1)
-            recv_a = lax.all_to_all(send_a, axes, 0, 0, tiled=True)
+            send_a = jnp.concatenate(
+                [rows_out.reshape(owners, 1, -1), outward.reshape(owners, 1, -1)], axis=2
+            )
+            recv_a = lax.all_to_all(send_a, axes, 0, 0, tiled=True).reshape(owners, -1)
             rows_in = recv_a[:, : CAP * 128].reshape(slots, 128)
             owned = coef_in(recv_a[:, CAP * 128 :])
 
@@ -342,9 +345,9 @@
         synth = legendre_pallas(owned, legendre, prior_gain, m_values, first_order)
         synth_send = synth.reshape(2, count_here, owners, cycles_here).transpose(2, 0, 1, 3)
         send_b = jnp.concatenate(
-            [binned_send.reshape(owners, CAP * 128), synth_send.reshape(owners, -1)], axis=1
+            [binned_send.reshape(owners, 1, CAP * 128), synth_send.reshape(owners, 1, -1)], axis=2
         )
-        recv_b = lax.all_to_all(send_b, axes, 0, 0, tiled=True)
+        recv_b = lax.all_to_all(send_b, axes, 0, 0, tiled=True).reshape(owners, -1)
         binned_in = recv_b[:, : CAP * 128].reshape(slots, 128)
         binned = jnp.dot(want_hot, binned_in, precision=highest).reshape(cycles_here, length)
         returned = recv_b[:, CAP * 128 :].reshape(owners, 2, count_here, cycles_here)

time: 168 us -> 170 us (1.012)
  other arithmetic: 12.5 us -> 16.6 us
  local copies, waits for them, and re-layouts: 23 us -> 20 us
    concatenate x0 -> x4, other arithmetic: none -> 5.11 us  [the longest x2 3.25 us: on_device(): jnp.concatenate([rows_out.reshape(owners, 1, -1), outward.reshape(owners,...]
    all_to_all x6 -> x1, other arithmetic: 5.07 us -> 1.72 us  [on_device(): lax.all_to_all(rows_out.reshape(owners, 1, -1), axes, 0, 0, tiled=True)]
    all_to_all x7 -> x3, local copies, waits for them, and re-layouts: 5.81 us -> 2.7 us  [the longest x2 1.79 us: on_device(): recv_b = lax.all_to_all(send_b, axes, 0, 0, tiled=True).reshape(owners, -1)]
    another operation x2 -> x4, other arithmetic: 0.8 us -> 3.2 us  [the longest x1 2.39 us: on_device(): rows_out.reshape(owners, 1, -1)]
where the time goes in v4:
time: 170 us; the launch traced here: 169 us
  Pallas kernels  38.5 us (23%)
  blocking collectives  34.4 us (20%)
  starting transfers between devices  25.6 us (15%)
  waiting for transfers between devices  22.1 us (13%)
  local copies, waits for them, and re-layouts  20 us (12%)
  other arithmetic  16.6 us (10%)
  matrix products  10 us (6%)
    pallas_call x2, Pallas kernels, legendre_pallas(): pl.pallas_call(functools.partial(legendre_body, scale=math.sqrt(total_cyc...  22.3 us
    all_to_all x1, blocking collectives, on_device(): recv_b = lax.all_to_all(send_b, axes, 0, 0, tiled=True).reshape(owners, -1)  18.5 us
    pallas_call x2, Pallas kernels, pointing_pallas(): pl.pallas_call(functools.partial(pointing_body, tblk=tblk, nsamp=nsamp),...  16.2 us
    all_to_all x1, blocking collectives, on_device(): recv_a = lax.all_to_all(send_a, axes, 0, 0, tiled=True).reshape(owners, -1)  15.9 us
    all_to_all x1, waiting for transfers between devices, on_device(): recv_b = lax.all_to_all(send_b, axes, 0, 0, tiled=True).reshape(owners, -1)  13.5 us
    all_to_all x1, starting transfers between devices, on_device(): info_recv = lax.all_to_all(info, axes, 0, 0, tiled=True)  11.5 us
    all_to_all x1, starting transfers between devices, on_device(): recv_b = lax.all_to_all(send_b, axes, 0, 0, tiled=True).reshape(owners, -1)  9.79 us
    all_to_all x1, waiting for transfers between devices, on_device(): info_recv = lax.all_to_all(info, axes, 0, 0, tiled=True)  8.61 us
  transfers between devices with their start and end apart: 3, of which 2 were waited for; matrix products, arithmetic and copies ran while one was open for 2% of the time, Pallas kernels for 7%

profile of v4, /device:TPU:1, one launch (start us, length us, event | category | flops | bytes accessed | tf_op | source)
XLA Modules:
  0.0 168.6 jit_solution(17519059360761134715)
XLA Ops:
  4.6 0.9 convolution_bitcast_fusion.3
  6.4 1.3 scatter_custom_fusion
  10.9 11.5 %all-to-all-start = ((f32[128,1,32]{2,1,0:T(1,128)}), f32[128,1,32]{2,1,0:T(1,128)S(1)}, u32[]{:S(2)}, u32[]{:S(2)}) async-start(f32[128,1,32]{2,1,0:T(1,128)} %bitcast.16), calls=%async_computation | async-start | bytes 131072 | tf_op jit(solution)/shard_map/all_to_all | solution.py:311
  23.6 8.6 %all-to-all-done = f32[128,1,32]{2,1,0:T(1,128)S(1)} async-done(((f32[128,1,32]{2,1,0:T(1,128)}), f32[128,1,32]{2,1,0:T(1,128)S(1)}, u32[]{:S(2)}, u32[]{:S(2)}) %all-to-all-start) | async-done | bytes 16416 | tf_op jit(solution)/shard_map/all_to_all | solution.py:311
  33.9 2.4 %reduce.17 = bf16[128,1024]{1,0:T(8,128)(2,1)S(1)} reduce(bf16[128,1,1024]{2,1,0:T(2,128)(2,1)S(1)} %reshape_reshape.12, bf16[]{:T(256)} %broadcast.976), dimensions={1}, to_apply=%reshape_reshape.12.reduce_sub_computation | reduce | bytes 524290 | tf_op jit(solution)/shard_map/reshape;reshape | solution.py:326
  37.1 4.3 %all-to-all-start.1 = ((bf16[128,2,512]{2,1,0:T(2,128)(2,1)}), bf16[128,2,512]{2,1,0:T(2,128)(2,1)S(1)}, u32[]{:S(2)}, u32[]{:S(2)}) async-start(bf16[128,2,512]{2,1,0:T(2,128)(2,1)} %reshape.1217), calls=%async_computation.1 | async-start | bytes 524288 | tf_op jit(solution)/shard_map/all_to_all | solution.py:326
  42.1 11.1 %shard_map.92 = f32[8,16,128]{2,1,0:T(8,128)} custom-call(s32[1]{0:T(128)} %bitcast.22.base_ref, s32[1024]{0:T(1024)} %m_ref.3, bf16[8,16,128]{2,1,0:T(8,128)(2,1)} %scatter.18.coef_ref, f32[1,6144]{1,0:T(1,128)} %bitcast.204, bf16[8,6144,128]{2,1,0:T(8,128)(2,1)} %tab_ref.3), custom_call_target="tpu_custom_call" | custom-call | tf_op jit(solution)/shard_map/pallas_call | solution.py:169
  54.3 1.7 %reduce.10 = bf16[128,1024]{1,0:T(8,128)(2,1)S(1)} reduce(bf16[128,1,1024]{2,1,0:T(2,128)(2,1)S(1)} %reshape.1218, bf16[]{:T(256)} %constant.213), dimensions={1}, to_apply=%all_to_all.23.reduce_sub_computation | reduce | bytes 524290 | tf_op jit(solution)/shard_map/all_to_all | solution.py:326
  56.1 1.0 convolution_convert_fusion.3
  57.1 8.1 %shard_map.91 = f32[4,64,128]{2,1,0:T(8,128)} custom-call(f32[4]{0:T(128)} %w_ref.3, bf16[4,64,128,128]{3,2,1,0:T(8,128)(2,1)} %p_ref.3, bf16[4,64,128]{2,1,0:T(8,128)(2,1)} %bitcast.207, f32[4,1,8192]{2,1,0:T(1,128)} %bitcast.192), custom_call_target="tpu_custom_call" | custom-call | tf_op jit(solution)/shard_map/pallas_call | solution.py:207
  65.2 2.0 %fusion.1 = f32[1024,128]{1,0:T(8,128)S(1)} fusion(f32[256,128]{1,0:T(8,128)} %bitcast.195, s32[256]{0:T(256)S(1)} %multiply_add_fusion.4), kind=kOutput, calls=%fused_computation.15 | convolution fusion | flops 402915328 | bytes 656384 | tf_op jit(solution)/shard_map/dot_general | solution.py:341
  67.2 1.3 pad_maximum_fusion
  68.5 9.8 %all-to-all-start.2 = ((f32[128,1,1040]{2,1,0:T(1,128)}), f32[128,1,1040]{2,1,0:T(1,128)S(1)}, u32[]{:S(2)}, u32[]{:S(2)}) async-start(f32[128,1,1040]{2,1,0:T(1,128)} %pad_maximum_fusion), calls=%async_computation.2 | async-start | bytes 1179648 | tf_op jit(solution)/shard_map/all_to_all | solution.py:350
  79.5 13.5 %all-to-all-done.2 = f32[128,1,1040]{2,1,0:T(1,128)S(1)} async-done(((f32[128,1,1040]{2,1,0:T(1,128)}), f32[128,1,1040]{2,1,0:T(1,128)S(1)}, u32[]{:S(2)}, u32[]{:S(2)}) %all-to-all-start.2) | async-done | bytes 532512 | tf_op jit(solution)/shard_map/all_to_all | solution.py:350
  93.1 0.9 copy.172
  100.8 2.6 %reduce.18 = bf16[128,1040]{1,0:T(8,128)(2,1)S(1)} reduce(bf16[128,1,1040]{2,1,0:T(2,128)(2,1)S(1)} %pad_maximum_fusion.1, bf16[]{:T(256)} %broadcast.976), dimensions={1}, to_apply=%pad_maximum_fusion.1.reduce_sub_computation | reduce | bytes 532482 | tf_op jit(solution)/shard_map/concatenate | solution.py:331
  103.7 15.9 %all_to_all.32 = bf16[128,2,520]{2,1,0:T(2,128)(2,1)S(1)} all-to-all(bf16[128,2,520]{2,1,0:T(2,128)(2,1)S(1)} %reshape.1219), channel_id=1, replica_groups=mesh['det'=8,'tm'=16] {'det','tm'}, dimensions={0} | all-to-all | bytes 532480 | tf_op jit(solution)/shard_map/all_to_all | solution.py:334
  120.1 0.9 copy.182
  121.4 1.0 convolution_convert_fusion.2
  123.0 11.2 %shard_map.94 = f32[8,16,128]{2,1,0:T(8,128)} custom-call(s32[1]{0:T(128)} %bitcast.22.base_ref, s32[1024]{0:T(1024)} %m_ref.3, bf16[8,16,128]{2,1,0:T(8,128)(2,1)} %scatter.19.coef_ref, f32[1,6144]{1,0:T(1,128)} %bitcast.205, bf16[8,6144,128]{2,1,0:T(8,128)(2,1)} %tab_ref.3), custom_call_target="tpu_custom_call" | custom-call | tf_op jit(solution)/shard_map/pallas_call | solution.py:169
  135.1 8.1 %shard_map.93 = f32[4,64,128]{2,1,0:T(8,128)} custom-call(f32[4]{0:T(128)} %w_ref.3, bf16[4,64,128,128]{3,2,1,0:T(8,128)(2,1)} %p_ref.3, bf16[4,64,128]{2,1,0:T(8,128)(2,1)} %bitcast.206, f32[4,1,8192]{2,1,0:T(1,128)} %bitcast.193), custom_call_target="tpu_custom_call" | custom-call | tf_op jit(solution)/shard_map/pallas_call | solution.py:207
  143.2 2.0 %fusion = f32[1024,128]{1,0:T(8,128)S(1)} fusion(f32[256,128]{1,0:T(8,128)} %bitcast.194, s32[256]{0:T(256)S(1)} %multiply_add_fusion.4), kind=kOutput, calls=%fused_computation.14 | convolution fusion | flops 402915328 | bytes 656384 | tf_op jit(solution)/shard_map/dot_general | solution.py:341
  145.7 18.5 %all_to_all.33 = f32[128,1,1040]{2,1,0:T(1,128)S(1)} all-to-all(f32[128,1,1040]{2,1,0:T(1,128)S(1)} %pad_maximum_fusion.2), channel_id=1, replica_groups=mesh['det'=8,'tm'=16] {'det','tm'}, dimensions={0} | all-to-all | bytes 1064960 | tf_op jit(solution)/shard_map/all_to_all | solution.py:350
  164.2 0.9 copy.188
  (140 shorter events, 27.8 us)
Async XLA Ops:
  10.9 21.3 %all-to-all-start = ((f32[128,1,32]{2,1,0:T(1,128)}), f32[128,1,32]{2,1,0:T(1,128)S(1)}, u32[]{:S(2)}, u32[]{:S(2)}) async-start(f32[128,1,32]{2,1,0:T(1,128)} %bitcast.16), calls=%async_computation | async-start | bytes 131072 | tf_op jit(solution)/shard_map/all_to_all | solution.py:311
  37.1 16.9 %all-to-all-start.1 = ((bf16[128,2,512]{2,1,0:T(2,128)(2,1)}), bf16[128,2,512]{2,1,0:T(2,128)(2,1)S(1)}, u32[]{:S(2)}, u32[]{:S(2)}) async-start(bf16[128,2,512]{2,1,0:T(2,128)(2,1)} %reshape.1217), calls=%async_computation.1 | async-start | bytes 524288 | tf_op jit(solution)/shard_map/all_to_all | solution.py:326
  53.2 41.9 %copy-start.1 = (s32[1024]{0:T(1024)S(1)}, s32[1024]{0:T(1024)}, u32[]{:S(2)}) copy-start(s32[1024]{0:T(1024)} %m_ref.3) | copy-start | bytes 12292
  53.2 43.7 %copy-start = (f32[1,8192]{1,0:T(1,128)S(1)}, f32[1,8192]{1,0:T(1,128)}, u32[]{:S(2)}) copy-start(f32[1,8192]{1,0:T(1,128)} %param.17) | copy-start | bytes 98308
  68.5 24.5 %all-to-all-start.2 = ((f32[128,1,1040]{2,1,0:T(1,128)}), f32[128,1,1040]{2,1,0:T(1,128)S(1)}, u32[]{:S(2)}, u32[]{:S(2)}) async-start(f32[128,1,1040]{2,1,0:T(1,128)} %pad_maximum_fusion), calls=%async_computation.2 | async-start | bytes 1179648 | tf_op jit(solution)/shard_map/all_to_all | solution.py:350
  123.0 43.2 %copy-start.2 = (s32[1024]{0:T(1024)S(1)}, s32[1024]{0:T(1024)}, u32[]{:S(2)}) copy-start(s32[1024]{0:T(1024)} %m_ref.3) | copy-start | bytes 12292

commit v5 on v4

--- a/solution.py
+++ b/solution.py
@@ -342,13 +342,25 @@
             slot_hot.T.astype(jnp.float32), binned_terms.reshape(-1, 128), precision=highest
         )
 
-        synth = legendre_pallas(owned, legendre, prior_gain, m_values, first_order)
-        synth_send = synth.reshape(2, count_here, owners, cycles_here).transpose(2, 0, 1, 3)
-        send_b = jnp.concatenate(
-            [binned_send.reshape(owners, 1, CAP * 128), synth_send.reshape(owners, 1, -1)], axis=2
-        )
-        recv_b = lax.all_to_all(send_b, axes, 0, 0, tiled=True).reshape(owners, -1)
-        binned_in = recv_b[:, : CAP * 128].reshape(slots, 128)
+        if iteration == ITERS - 1:
+            binned_in = lax.all_to_all(
+                binned_send.reshape(owners, 1, CAP * 128), axes, 0, 0, tiled=True
+            ).reshape(slots, 128)
+            synth = legendre_pallas(owned, legendre, prior_gain, m_values, first_order)
+            synth_send = synth.reshape(2, count_here, owners, cycles_here).transpose(2, 0, 1, 3)
+            recv_b = lax.all_to_all(synth_send.reshape(owners, 1, -1), axes, 0, 0, tiled=True)
+            recv_b = jnp.concatenate(
+                [jnp.zeros((owners, CAP * 128), jnp.float32), recv_b.reshape(owners, -1)], axis=1
+            )
+        else:
+            synth = legendre_pallas(owned, legendre, prior_gain, m_values, first_order)
+            synth_send = synth.reshape(2, count_here, owners, cycles_here).transpose(2, 0, 1, 3)
+            send_b = jnp.concatenate(
+                [binned_send.reshape(owners, 1, CAP * 128), synth_send.reshape(owners, 1, -1)],
+                axis=2,
+            )
+            recv_b = lax.all_to_all(send_b, axes, 0, 0, tiled=True).reshape(owners, -1)
+            binned_in = recv_b[:, : CAP * 128].reshape(slots, 128)
         binned = jnp.dot(want_hot, binned_in, precision=highest).reshape(cycles_here, length)
         returned = recv_b[:, CAP * 128 :].reshape(owners, 2, count_here, cycles_here)
         returned = returned.transpose(1, 0, 2, 3).reshape(2, owners * count_here, cycles_here)

time: 170 us -> 177 us (1.041)
  blocking collectives: 34.4 us -> 15.9 us
  starting transfers between devices: 25.6 us -> 39.3 us
  waiting for transfers between devices: 22.1 us -> 34.1 us
    all_to_all x1 -> x0, blocking collectives: 18.5 us -> none  [on_device(): recv_b = lax.all_to_all(send_b, axes, 0, 0, tiled=True).reshape(owners, -1)]
    all_to_all x0 -> x2, starting transfers between devices: none -> 13.8 us  [the longest x1 9.78 us: on_device(): lax.all_to_all(binned_send.reshape(owners, 1, CAP * 128), axes, 0, 0, til...]
    all_to_all x0 -> x2, waiting for transfers between devices: none -> 11.9 us  [the longest x1 11.9 us: on_device(): lax.all_to_all(binned_send.reshape(owners, 1, CAP * 128), axes, 0, 0, til...]
  transfers between devices with their start and end apart: 3 -> 5, of which waited for: 2 -> 3; matrix products, arithmetic and copies ran while one was open for 2% -> 5% of each run, Pallas kernels for 7% -> 11%
where the time goes in v5:
time: 177 us; the launch traced here: 175 us
  starting transfers between devices  39.3 us (22%)
  Pallas kernels  38.3 us (22%)
  waiting for transfers between devices  34.1 us (19%)
  local copies, waits for them, and re-layouts  19.5 us (11%)
  other arithmetic  16.1 us (9%)
  blocking collectives  15.9 us (9%)
  matrix products  10.8 us (6%)
    pallas_call x2, Pallas kernels, legendre_pallas(): pl.pallas_call(functools.partial(legendre_body, scale=math.sqrt(total_cyc...  22.1 us
    pallas_call x2, Pallas kernels, pointing_pallas(): pl.pallas_call(functools.partial(pointing_body, tblk=tblk, nsamp=nsamp),...  16.2 us
    all_to_all x1, blocking collectives, on_device(): recv_a = lax.all_to_all(send_a, axes, 0, 0, tiled=True).reshape(owners, -1)  15.9 us
    all_to_all x1, waiting for transfers between devices, on_device(): recv_b = lax.all_to_all(send_b, axes, 0, 0, tiled=True).reshape(owners, -1)  13.5 us
    all_to_all x1, waiting for transfers between devices, on_device(): lax.all_to_all(binned_send.reshape(owners, 1, CAP * 128), axes, 0, 0, til...  11.9 us
    all_to_all x1, starting transfers between devices, on_device(): info_recv = lax.all_to_all(info, axes, 0, 0, tiled=True)  11.5 us
    all_to_all x1, starting transfers between devices, on_device(): recv_b = lax.all_to_all(send_b, axes, 0, 0, tiled=True).reshape(owners, -1)  9.78 us
    all_to_all x1, starting transfers between devices, on_device(): lax.all_to_all(binned_send.reshape(owners, 1, CAP * 128), axes, 0, 0, til...  9.78 us
  transfers between devices with their start and end apart: 5, of which 3 were waited for; matrix products, arithmetic and copies ran while one was open for 5% of the time, Pallas kernels for 11%

profile of v5, /device:TPU:1, one launch (start us, length us, event | category | flops | bytes accessed | tf_op | source)
XLA Modules:
  0.0 175.3 jit_solution(8371582440589785894)
XLA Ops:
  4.6 0.9 convolution_bitcast_fusion.3
  6.4 1.3 scatter_custom_fusion
  10.9 11.5 %all-to-all-start = ((f32[128,1,32]{2,1,0:T(1,128)}), f32[128,1,32]{2,1,0:T(1,128)S(1)}, u32[]{:S(2)}, u32[]{:S(2)}) async-start(f32[128,1,32]{2,1,0:T(1,128)} %bitcast.16), calls=%async_computation | async-start | bytes 131072 | tf_op jit(solution)/shard_map/all_to_all | solution.py:311
  23.6 8.6 %all-to-all-done = f32[128,1,32]{2,1,0:T(1,128)S(1)} async-done(((f32[128,1,32]{2,1,0:T(1,128)}), f32[128,1,32]{2,1,0:T(1,128)S(1)}, u32[]{:S(2)}, u32[]{:S(2)}) %all-to-all-start) | async-done | bytes 16416 | tf_op jit(solution)/shard_map/all_to_all | solution.py:311
  33.9 2.4 %reduce.17 = bf16[128,1024]{1,0:T(8,128)(2,1)S(1)} reduce(bf16[128,1,1024]{2,1,0:T(2,128)(2,1)S(1)} %reshape_reshape.16, bf16[]{:T(256)} %broadcast.976), dimensions={1}, to_apply=%reshape_reshape.16.reduce_sub_computation | reduce | bytes 524290 | tf_op jit(solution)/shard_map/reshape;reshape | solution.py:326
  37.1 4.3 %all-to-all-start.1 = ((bf16[128,2,512]{2,1,0:T(2,128)(2,1)}), bf16[128,2,512]{2,1,0:T(2,128)(2,1)S(1)}, u32[]{:S(2)}, u32[]{:S(2)}) async-start(bf16[128,2,512]{2,1,0:T(2,128)(2,1)} %reshape.1209), calls=%async_computation.1 | async-start | bytes 524288 | tf_op jit(solution)/shard_map/all_to_all | solution.py:326
  42.1 11.1 %shard_map.92 = f32[8,16,128]{2,1,0:T(8,128)} custom-call(s32[1]{0:T(128)} %bitcast.22.base_ref, s32[1024]{0:T(1024)} %m_ref.3, bf16[8,16,128]{2,1,0:T(8,128)(2,1)} %scatter.18.coef_ref, f32[1,6144]{1,0:T(1,128)} %bitcast.201, bf16[8,6144,128]{2,1,0:T(8,128)(2,1)} %tab_ref.3), custom_call_target="tpu_custom_call" | custom-call | tf_op jit(solution)/shard_map/pallas_call | solution.py:169
  54.3 1.7 reduce.10
  56.1 1.0 convolution_convert_fusion.3
  57.1 8.1 %shard_map.91 = f32[4,64,128]{2,1,0:T(8,128)} custom-call(f32[4]{0:T(128)} %w_ref.3, bf16[4,64,128,128]{3,2,1,0:T(8,128)(2,1)} %p_ref.3, bf16[4,64,128]{2,1,0:T(8,128)(2,1)} %bitcast.204, f32[4,1,8192]{2,1,0:T(1,128)} %bitcast.189), custom_call_target="tpu_custom_call" | custom-call | tf_op jit(solution)/shard_map/pallas_call | solution.py:207
  65.2 2.0 %fusion.1 = f32[1024,128]{1,0:T(8,128)S(1)} fusion(f32[256,128]{1,0:T(8,128)} %bitcast.192, s32[256]{0:T(256)S(1)} %multiply_add_fusion.4), kind=kOutput, calls=%fused_computation.15 | convolution fusion | flops 402915328 | bytes 656384 | tf_op jit(solution)/shard_map/dot_general | solution.py:341
  67.2 1.3 pad_maximum_fusion
  68.5 9.8 %all-to-all-start.2 = ((f32[128,1,1040]{2,1,0:T(1,128)}), f32[128,1,1040]{2,1,0:T(1,128)S(1)}, u32[]{:S(2)}, u32[]{:S(2)}) async-start(f32[128,1,1040]{2,1,0:T(1,128)} %pad_maximum_fusion), calls=%async_computation.2 | async-start | bytes 1179648 | tf_op jit(solution)/shard_map/all_to_all | solution.py:362
  79.5 13.5 %all-to-all-done.2 = f32[128,1,1040]{2,1,0:T(1,128)S(1)} async-done(((f32[128,1,1040]{2,1,0:T(1,128)}), f32[128,1,1040]{2,1,0:T(1,128)S(1)}, u32[]{:S(2)}, u32[]{:S(2)}) %all-to-all-start.2) | async-done | bytes 532512 | tf_op jit(solution)/shard_map/all_to_all | solution.py:362
  100.8 2.6 %reduce.18 = bf16[128,1040]{1,0:T(8,128)(2,1)S(1)} reduce(bf16[128,1,1040]{2,1,0:T(2,128)(2,1)S(1)} %pad_maximum_fusion.1, bf16[]{:T(256)} %broadcast.976), dimensions={1}, to_apply=%pad_maximum_fusion.1.reduce_sub_computation | reduce | bytes 532482 | tf_op jit(solution)/shard_map/concatenate | solution.py:331
  103.7 15.9 %all_to_all.37 = bf16[128,2,520]{2,1,0:T(2,128)(2,1)S(1)} all-to-all(bf16[128,2,520]{2,1,0:T(2,128)(2,1)S(1)} %reshape.1211), channel_id=1, replica_groups=mesh['det'=8,'tm'=16] {'det','tm'}, dimensions={0} | all-to-all | bytes 532480 | tf_op jit(solution)/shard_map/all_to_all | solution.py:334
  120.1 0.9 copy.176
  121.4 1.0 convolution_convert_fusion.2
  123.0 11.1 %shard_map.94 = f32[8,16,128]{2,1,0:T(8,128)} custom-call(s32[1]{0:T(128)} %bitcast.22.base_ref, s32[1024]{0:T(1024)} %m_ref.3, bf16[8,16,128]{2,1,0:T(8,128)(2,1)} %scatter.19.coef_ref, f32[1,6144]{1,0:T(1,128)} %bitcast.202, bf16[8,6144,128]{2,1,0:T(8,128)(2,1)} %tab_ref.3), custom_call_target="tpu_custom_call" | custom-call | tf_op jit(solution)/shard_map/pallas_call | solution.py:169
  135.5 4.0 %all-to-all-start.5 = ((f32[128,1,16]{2,1,0:T(1,128)}), f32[128,1,16]{2,1,0:T(1,128)S(1)}, u32[]{:S(2)}, u32[]{:S(2)}) async-start(f32[128,1,16]{2,1,0:T(1,128)} %copy.181), calls=%async_computation.5 | async-start | bytes 131072 | tf_op jit(solution)/shard_map/all_to_all | solution.py:351
  139.5 8.1 %shard_map.93 = f32[4,64,128]{2,1,0:T(8,128)} custom-call(f32[4]{0:T(128)} %w_ref.3, bf16[4,64,128,128]{3,2,1,0:T(8,128)(2,1)} %p_ref.3, bf16[4,64,128]{2,1,0:T(8,128)(2,1)} %bitcast.203, f32[4,1,8192]{2,1,0:T(1,128)} %bitcast.190), custom_call_target="tpu_custom_call" | custom-call | tf_op jit(solution)/shard_map/pallas_call | solution.py:207
  147.6 2.8 %fusion = f32[1024,128]{1,0:T(8,128)} fusion(f32[256,128]{1,0:T(8,128)} %bitcast.191, s32[256]{0:T(256)S(1)} %multiply_add_fusion.4), kind=kOutput, calls=%fused_computation.14 | convolution fusion | flops 402915328 | bytes 656384 | tf_op jit(solution)/shard_map/dot_general | solution.py:341
  150.4 9.8 %all-to-all-start.4 = ((f32[128,1,1024]{2,1,0:T(1,128)}), f32[128,1,1024]{2,1,0:T(1,128)S(1)}, u32[]{:S(2)}, u32[]{:S(2)}) async-start(f32[128,1,1024]{2,1,0:T(1,128)} %bitcast.59), calls=%async_computation.4 | async-start | bytes 1048576 | tf_op jit(solution)/shard_map/all_to_all | solution.py:346
  162.4 11.9 %all-to-all-done.4 = f32[128,1,1024]{2,1,0:T(1,128)S(1)} async-done(((f32[128,1,1024]{2,1,0:T(1,128)}), f32[128,1,1024]{2,1,0:T(1,128)S(1)}, u32[]{:S(2)}, u32[]{:S(2)}) %all-to-all-start.4) | async-done | bytes 524320 | tf_op jit(solution)/shard_map/all_to_all | solution.py:346
  (138 shorter events, 28.5 us)
Async XLA Ops:
  10.9 21.3 %all-to-all-start = ((f32[128,1,32]{2,1,0:T(1,128)}), f32[128,1,32]{2,1,0:T(1,128)S(1)}, u32[]{:S(2)}, u32[]{:S(2)}) async-start(f32[128,1,32]{2,1,0:T(1,128)} %bitcast.16), calls=%async_computation | async-start | bytes 131072 | tf_op jit(solution)/shard_map/all_to_all | solution.py:311
  37.1 16.9 %all-to-all-start.1 = ((bf16[128,2,512]{2,1,0:T(2,128)(2,1)}), bf16[128,2,512]{2,1,0:T(2,128)(2,1)S(1)}, u32[]{:S(2)}, u32[]{:S(2)}) async-start(bf16[128,2,512]{2,1,0:T(2,128)(2,1)} %reshape.1209), calls=%async_computation.1 | async-start | bytes 524288 | tf_op jit(solution)/shard_map/all_to_all | solution.py:326
  53.2 41.9 %copy-start.1 = (s32[1024]{0:T(1024)S(1)}, s32[1024]{0:T(1024)}, u32[]{:S(2)}) copy-start(s32[1024]{0:T(1024)} %m_ref.3) | copy-start | bytes 12292
  53.2 43.7 %copy-start = (f32[1,8192]{1,0:T(1,128)S(1)}, f32[1,8192]{1,0:T(1,128)}, u32[]{:S(2)}) copy-start(f32[1,8192]{1,0:T(1,128)} %param.17) | copy-start | bytes 98308
  68.5 24.5 %all-to-all-start.2 = ((f32[128,1,1040]{2,1,0:T(1,128)}), f32[128,1,1040]{2,1,0:T(1,128)S(1)}, u32[]{:S(2)}, u32[]{:S(2)}) async-start(f32[128,1,1040]{2,1,0:T(1,128)} %pad_maximum_fusion), calls=%async_computation.2 | async-start | bytes 1179648 | tf_op jit(solution)/shard_map/all_to_all | solution.py:362
  121.2 39.4 %copy-start.2 = (s32[1024]{0:T(1024)S(1)}, s32[1024]{0:T(1024)}, u32[]{:S(2)}) copy-start(s32[1024]{0:T(1024)} %m_ref.3) | copy-start | bytes 12292
  135.5 14.9 %all-to-all-start.5 = ((f32[128,1,16]{2,1,0:T(1,128)}), f32[128,1,16]{2,1,0:T(1,128)S(1)}, u32[]{:S(2)}, u32[]{:S(2)}) async-start(f32[128,1,16]{2,1,0:T(1,128)} %copy.181), calls=%async_computation.5 | async-start | bytes 131072 | tf_op jit(solution)/shard_map/all_to_all | solution.py:351
  150.4 23.9 %all-to-all-start.4 = ((f32[128,1,1024]{2,1,0:T(1,128)}), f32[128,1,1024]{2,1,0:T(1,128)S(1)}, u32[]{:S(2)}, u32[]{:S(2)}) async-start(f32[128,1,1024]{2,1,0:T(1,128)} %bitcast.59), calls=%async_computation.4 | async-start | bytes 1048576 | tf_op jit(solution)/shard_map/all_to_all | solution.py:346

commit v6 on v2

--- a/solution.py
+++ b/solution.py
@@ -137,37 +137,39 @@
 ROWS = 16
 
 
-def legendre_body(m_ref, coef_ref, gain_ref, tab_ref, out_ref, *, scale):
+def legendre_body(m_ref, coef_ref, gain_ref, tab_ref, out_ref, *, scale, per):
     k = pl.program_id(0)
-    tab = tab_ref[0]
-    coef = coef_ref[0]
-    analysed = lax.dot_general(
-        coef, tab, (((1,), (1,)), ((), ())), preferred_element_type=jnp.float32
-    )
-    degree = lax.broadcasted_iota(jnp.int32, analysed.shape, 1)
-    keep = degree >= m_ref[k]
-    scaled = jnp.where(keep, analysed * gain_ref[...], 0.0).astype(jnp.bfloat16)
-    synth = jnp.dot(scaled, tab, preferred_element_type=jnp.float32)
-    out_ref[0] = synth * scale
+    for j in range(per):
+        tab = tab_ref[j]
+        coef = coef_ref[j]
+        analysed = lax.dot_general(
+            coef, tab, (((1,), (1,)), ((), ())), preferred_element_type=jnp.float32
+        )
+        degree = lax.broadcasted_iota(jnp.int32, analysed.shape, 1)
+        keep = degree >= m_ref[k * per + j]
+        scaled = jnp.where(keep, analysed * gain_ref[...], 0.0).astype(jnp.bfloat16)
+        synth = jnp.dot(scaled, tab, preferred_element_type=jnp.float32)
+        out_ref[j] = synth * scale
 
 
 def legendre_pallas(owned, legendre, prior_gain, m_own):
     count_here, degrees, total_cycles = legendre.shape
+    per = 2 if count_here % 2 == 0 else 1
     coef = jnp.zeros((count_here, ROWS, total_cycles), jnp.bfloat16)
     coef = coef.at[:, :2, :].set(owned.transpose(1, 0, 2))
     gain = prior_gain.reshape(1, degrees)
     grid_spec = pltpu.PrefetchScalarGridSpec(
         num_scalar_prefetch=1,
-        grid=(count_here,),
+        grid=(count_here // per,),
         in_specs=[
-            pl.BlockSpec((1, ROWS, total_cycles), lambda k, m: (k, 0, 0)),
+            pl.BlockSpec((per, ROWS, total_cycles), lambda k, m: (k, 0, 0)),
             pl.BlockSpec((1, degrees), lambda k, m: (0, 0)),
-            pl.BlockSpec((1, degrees, total_cycles), lambda k, m: (k, 0, 0)),
+            pl.BlockSpec((per, degrees, total_cycles), lambda k, m: (k, 0, 0)),
         ],
-        out_specs=pl.BlockSpec((1, ROWS, total_cycles), lambda k, m: (k, 0, 0)),
+        out_specs=pl.BlockSpec((per, ROWS, total_cycles), lambda k, m: (k, 0, 0)),
     )
     out = pl.pallas_call(
-        functools.partial(legendre_body, scale=math.sqrt(total_cycles / degrees)),
+        functools.partial(legendre_body, scale=math.sqrt(total_cycles / degrees), per=per),
         grid_spec=grid_spec,
         out_shape=jax.ShapeDtypeStruct((count_here, ROWS, total_cycles), jnp.float32),
     )(m_own, coef, gain, legendre)

time: 168 us -> 164 us (0.976)
  Pallas kernels: 38.2 us -> 34.8 us
    pallas_call x2, Pallas kernels: 22 us -> 18.6 us  [legendre_pallas(): pl.pallas_call(functools.partial(legendre_body, scale=math.sqrt(total_cyc...]
  transfers between devices with their start and end apart: 3 -> 3, of which waited for: 2 -> 3; matrix products, arithmetic and copies ran while one was open for 3% -> 3% of each run, Pallas kernels for 7% -> 6%
where the time goes in v6:
time: 164 us; the launch traced here: 163 us
  Pallas kernels  34.8 us (21%)
  blocking collectives  34.4 us (21%)
  local copies, waits for them, and re-layouts  29.9 us (18%)
  starting transfers between devices  25 us (15%)
  waiting for transfers between devices  21.4 us (13%)
  other arithmetic  12.1 us (7%)
  matrix products  4.12 us (3%)
    pallas_call x2, Pallas kernels, legendre_pallas(): pl.pallas_call(functools.partial(legendre_body, scale=math.sqrt(total_cyc...  18.6 us
    all_to_all x1, blocking collectives, on_device(): recv_b = lax.all_to_all(send_b, axes, 0, 0, tiled=True)  18.5 us
    pallas_call x2, Pallas kernels, pointing_pallas(): pl.pallas_call(functools.partial(pointing_body, tblk=tblk, nsamp=nsamp),...  16.2 us
    all_to_all x1, blocking collectives, on_device(): recv_a = lax.all_to_all(send_a, axes, 0, 0, tiled=True)  15.9 us
    all_to_all x1, waiting for transfers between devices, on_device(): recv_b = lax.all_to_all(send_b, axes, 0, 0, tiled=True)  13.5 us
    all_to_all x1, starting transfers between devices, on_device(): info_recv = lax.all_to_all(info, axes, 0, 0, tiled=True)  11.5 us
    all_to_all x1, starting transfers between devices, on_device(): recv_b = lax.all_to_all(send_b, axes, 0, 0, tiled=True)  9.17 us
    all_to_all x1, waiting for transfers between devices, on_device(): info_recv = lax.all_to_all(info, axes, 0, 0, tiled=True)  7.27 us
  transfers between devices with their start and end apart: 3, of which 3 were waited for; matrix products, arithmetic and copies ran while one was open for 3% of the time, Pallas kernels for 6%

profile of v6, /device:TPU:1, one launch (start us, length us, event | category | flops | bytes accessed | tf_op | source)
XLA Modules:
  0.0 163.1 jit_solution(8088984171442269441)
XLA Ops:
  4.6 0.9 convolution_bitcast_fusion.3
  6.4 1.3 scatter_custom_fusion
  10.9 11.5 %all-to-all-start = ((f32[128,1,32]{2,1,0:T(1,128)}), f32[128,1,32]{2,1,0:T(1,128)S(1)}, u32[]{:S(2)}, u32[]{:S(2)}) async-start(f32[128,1,32]{2,1,0:T(1,128)} %bitcast.16), calls=%async_computation | async-start | bytes 131072 | tf_op jit(solution)/shard_map/all_to_all | solution.py:312
  23.6 1.3 dynamic_slice.3.m_ref
  25.0 7.3 %all-to-all-done = f32[128,1,32]{2,1,0:T(1,128)S(1)} async-done(((f32[128,1,32]{2,1,0:T(1,128)}), f32[128,1,32]{2,1,0:T(1,128)S(1)}, u32[]{:S(2)}, u32[]{:S(2)}) %all-to-all-start) | async-done | bytes 16416 | tf_op jit(solution)/shard_map/all_to_all | solution.py:312
  33.9 2.2 %reduce.17 = bf16[128,1024]{1,0:T(8,128)(2,1)S(1)} reduce(bf16[128,1,1024]{2,1,0:T(2,128)(2,1)S(1)} %all_to_all.52, bf16[]{:T(256)} %broadcast.972), dimensions={1}, to_apply=%all_to_all.52.reduce_sub_computation | reduce | bytes 524290 | tf_op jit(solution)/shard_map/all_to_all | solution.py:327
  37.0 4.3 %all-to-all-start.1 = ((bf16[128,2,512]{2,1,0:T(2,128)(2,1)}), bf16[128,2,512]{2,1,0:T(2,128)(2,1)S(1)}, u32[]{:S(2)}, u32[]{:S(2)}) async-start(bf16[128,2,512]{2,1,0:T(2,128)(2,1)} %reshape.1249), calls=%async_computation.1 | async-start | bytes 524288 | tf_op jit(solution)/shard_map/all_to_all | solution.py:327
  41.9 9.3 %shard_map.92 = f32[8,16,128]{2,1,0:T(8,128)} custom-call(s32[8]{0:T(128)} %dynamic_slice.3.m_ref, bf16[8,16,128]{2,1,0:T(8,128)(2,1)} %scatter.33.coef_ref, f32[1,6144]{1,0:T(1,128)} %bitcast.205, bf16[8,6144,128]{2,1,0:T(8,128)(2,1)} %tab_ref.3), custom_call_target="tpu_custom_call" | custom-call | tf_op jit(solution)/shard_map/pallas_call | solution.py:171
  53.0 1.5 reduce.10
  54.6 1.5 gather_fusion
  56.1 8.1 %shard_map.91 = f32[4,64,128]{2,1,0:T(8,128)} custom-call(f32[4]{0:T(128)} %w_ref.3, bf16[4,64,128,128]{3,2,1,0:T(8,128)(2,1)} %p_ref.3, bf16[4,64,128]{2,1,0:T(8,128)(2,1)} %bitcast.198, f32[4,1,8192]{2,1,0:T(1,128)} %bitcast.191), custom_call_target="tpu_custom_call" | custom-call | tf_op jit(solution)/shard_map/pallas_call | solution.py:209
  64.2 1.6 %scatter_custom_fusion.1 = f32[1024,128]{1,0:T(8,128)S(1)} fusion(s32[256]{0:T(256)S(1)} %bitcast.215, f32[256,128]{1,0:T(8,128)} %bitcast.200, f32[]{:T(128)} %constant.173.clone.1), kind=kCustom, calls=%fused_computation.33 | custom fusion | bytes 524800 | tf_op jit(solution)/shard_map/scatter | solution.py:338
  66.0 1.4 copy.135
  67.4 9.2 %all-to-all-start.2 = ((f32[128,1,1040]{2,1,0:T(1,128)}), f32[128,1,1040]{2,1,0:T(1,128)S(1)}, u32[]{:S(2)}, u32[]{:S(2)}) async-start(f32[128,1,1040]{2,1,0:T(1,128)} %copy.135), calls=%async_computation.2 | async-start | bytes 1179648 | tf_op jit(solution)/shard_map/all_to_all | solution.py:345
  77.8 13.5 %all-to-all-done.2 = f32[128,1,1040]{2,1,0:T(1,128)S(1)} async-done(((f32[128,1,1040]{2,1,0:T(1,128)}), f32[128,1,1040]{2,1,0:T(1,128)S(1)}, u32[]{:S(2)}, u32[]{:S(2)}) %all-to-all-start.2) | async-done | bytes 532512 | tf_op jit(solution)/shard_map/all_to_all | solution.py:345
  91.3 0.9 copy.136
  99.8 15.9 %all_to_all.58 = bf16[128,2,520]{2,1,0:T(2,128)(2,1)S(1)} all-to-all(bf16[128,2,520]{2,1,0:T(2,128)(2,1)S(1)} %reshape.1251), channel_id=1, replica_groups=mesh['det'=8,'tm'=16] {'det','tm'}, dimensions={0} | all-to-all | bytes 532480 | tf_op jit(solution)/shard_map/all_to_all | solution.py:332
  116.2 0.9 copy.146
  117.4 1.5 gather_fusion.1
  119.5 9.3 %shard_map.94 = f32[8,16,128]{2,1,0:T(8,128)} custom-call(s32[8]{0:T(128)} %dynamic_slice.3.m_ref, bf16[8,16,128]{2,1,0:T(8,128)(2,1)} %scatter.35.coef_ref, f32[1,6144]{1,0:T(1,128)} %bitcast.206, bf16[8,6144,128]{2,1,0:T(8,128)(2,1)} %tab_ref.3), custom_call_target="tpu_custom_call" | custom-call | tf_op jit(solution)/shard_map/pallas_call | solution.py:171
  129.7 8.1 %shard_map.93 = f32[4,64,128]{2,1,0:T(8,128)} custom-call(f32[4]{0:T(128)} %w_ref.3, bf16[4,64,128,128]{3,2,1,0:T(8,128)(2,1)} %p_ref.3, bf16[4,64,128]{2,1,0:T(8,128)(2,1)} %bitcast.197, f32[4,1,8192]{2,1,0:T(1,128)} %bitcast.192), custom_call_target="tpu_custom_call" | custom-call | tf_op jit(solution)/shard_map/pallas_call | solution.py:209
  137.8 1.6 %scatter_custom_fusion.2 = f32[1024,128]{1,0:T(8,128)S(1)} fusion(s32[256]{0:T(256)S(1)} %bitcast.216, f32[256,128]{1,0:T(8,128)} %bitcast.199, f32[]{:T(128)} %constant.173.clone.1), kind=kCustom, calls=%fused_computation.31 | custom fusion | bytes 524800 | tf_op jit(solution)/shard_map/scatter | solution.py:338
  140.2 18.5 %all_to_all.59 = f32[128,1,1040]{2,1,0:T(1,128)S(1)} all-to-all(f32[128,1,1040]{2,1,0:T(1,128)S(1)} %copy.151), channel_id=1, replica_groups=mesh['det'=8,'tm'=16] {'det','tm'}, dimensions={0} | all-to-all | bytes 1064960 | tf_op jit(solution)/shard_map/all_to_all | solution.py:345
  158.7 0.9 copy.152
  (144 shorter events, 29.1 us)
Async XLA Ops:
  10.9 21.3 %all-to-all-start = ((f32[128,1,32]{2,1,0:T(1,128)}), f32[128,1,32]{2,1,0:T(1,128)S(1)}, u32[]{:S(2)}, u32[]{:S(2)}) async-start(f32[128,1,32]{2,1,0:T(1,128)} %bitcast.16), calls=%async_computation | async-start | bytes 131072 | tf_op jit(solution)/shard_map/all_to_all | solution.py:312
  37.0 15.8 %all-to-all-start.1 = ((bf16[128,2,512]{2,1,0:T(2,128)(2,1)}), bf16[128,2,512]{2,1,0:T(2,128)(2,1)S(1)}, u32[]{:S(2)}, u32[]{:S(2)}) async-start(bf16[128,2,512]{2,1,0:T(2,128)(2,1)} %reshape.1249), calls=%async_computation.1 | async-start | bytes 524288 | tf_op jit(solution)/shard_map/all_to_all | solution.py:327
  51.2 42.1 %copy-start.1 = (s32[1024]{0:T(1024)S(1)}, s32[1024]{0:T(1024)}, u32[]{:S(2)}) copy-start(s32[1024]{0:T(1024)} %param.20) | copy-start | bytes 12292
  52.9 42.2 %copy-start = (f32[1,8192]{1,0:T(1,128)S(1)}, f32[1,8192]{1,0:T(1,128)}, u32[]{:S(2)}) copy-start(f32[1,8192]{1,0:T(1,128)} %param.17) | copy-start | bytes 98308
  67.4 23.9 %all-to-all-start.2 = ((f32[128,1,1040]{2,1,0:T(1,128)}), f32[128,1,1040]{2,1,0:T(1,128)S(1)}, u32[]{:S(2)}, u32[]{:S(2)}) async-start(f32[128,1,1040]{2,1,0:T(1,128)} %copy.135), calls=%async_computation.2 | async-start | bytes 1179648 | tf_op jit(solution)/shard_map/all_to_all | solution.py:345

commit v7 on v6

--- a/solution.py
+++ b/solution.py
@@ -155,8 +155,7 @@
 def legendre_pallas(owned, legendre, prior_gain, m_own):
     count_here, degrees, total_cycles = legendre.shape
     per = 2 if count_here % 2 == 0 else 1
-    coef = jnp.zeros((count_here, ROWS, total_cycles), jnp.bfloat16)
-    coef = coef.at[:, :2, :].set(owned.transpose(1, 0, 2))
+    coef = jnp.pad(owned.transpose(1, 0, 2), ((0, 0), (0, ROWS - 2), (0, 0)))
     gain = prior_gain.reshape(1, degrees)
     grid_spec = pltpu.PrefetchScalarGridSpec(
         num_scalar_prefetch=1,
@@ -176,38 +175,40 @@
     return out[:, :2, :].transpose(1, 0, 2)
 
 
-def pointing_body(w_ref, p_ref, x_ref, s_ref, out_ref, *, tblk, nsamp):
+def pointing_body(w_ref, p_ref, x_ref, s_ref, out_ref, *, tblk, nsamp, per):
     d = pl.program_id(0)
-    point = p_ref[0].reshape(tblk * nsamp, p_ref.shape[3])
-    picked = x_ref[0]
-    every = lax.dot_general(
-        picked, point, (((1,), (1,)), ((), ())), preferred_element_type=jnp.float32
-    )
-    row = lax.broadcasted_iota(jnp.int32, every.shape, 0)
-    col = lax.broadcasted_iota(jnp.int32, every.shape, 1)
-    mine = row == col // nsamp
-    predicted = jnp.sum(jnp.where(mine, every, 0.0), axis=0, keepdims=True)
-    resid = (w_ref[d] * (s_ref[0] - predicted)).astype(jnp.bfloat16)
-    spread = jnp.where(mine, jnp.broadcast_to(resid, every.shape), jnp.zeros_like(resid))
-    out_ref[0] = jnp.dot(spread, point, preferred_element_type=jnp.float32)
+    for j in range(per):
+        point = p_ref[j].reshape(tblk * nsamp, p_ref.shape[3])
+        picked = x_ref[j]
+        every = lax.dot_general(
+            picked, point, (((1,), (1,)), ((), ())), preferred_element_type=jnp.float32
+        )
+        row = lax.broadcasted_iota(jnp.int32, every.shape, 0)
+        col = lax.broadcasted_iota(jnp.int32, every.shape, 1)
+        mine = row == col // nsamp
+        predicted = jnp.sum(jnp.where(mine, every, 0.0), axis=0, keepdims=True)
+        resid = (w_ref[d * per + j] * (s_ref[j] - predicted)).astype(jnp.bfloat16)
+        spread = jnp.where(mine, jnp.broadcast_to(resid, every.shape), jnp.zeros_like(resid))
+        out_ref[j] = jnp.dot(spread, point, preferred_element_type=jnp.float32)
 
 
 def pointing_pallas(pointing, picked, samples, det_weight):
     dets, times, nsamp, npix = pointing.shape
     tblk = times
+    per = 2 if dets % 2 == 0 else 1
     samples_row = samples.reshape(dets, 1, times * nsamp)
     grid_spec = pltpu.PrefetchScalarGridSpec(
         num_scalar_prefetch=1,
-        grid=(dets, times // tblk),
+        grid=(dets // per,),
         in_specs=[
-            pl.BlockSpec((1, tblk, nsamp, npix), lambda d, t, w: (d, t, 0, 0)),
-            pl.BlockSpec((1, tblk, npix), lambda d, t, w: (d, t, 0)),
-            pl.BlockSpec((1, 1, tblk * nsamp), lambda d, t, w: (d, 0, t)),
+            pl.BlockSpec((per, tblk, nsamp, npix), lambda d, w: (d, 0, 0, 0)),
+            pl.BlockSpec((per, tblk, npix), lambda d, w: (d, 0, 0)),
+            pl.BlockSpec((per, 1, tblk * nsamp), lambda d, w: (d, 0, 0)),
         ],
-        out_specs=pl.BlockSpec((1, tblk, npix), lambda d, t, w: (d, t, 0)),
+        out_specs=pl.BlockSpec((per, tblk, npix), lambda d, w: (d, 0, 0)),
     )
     return pl.pallas_call(
-        functools.partial(pointing_body, tblk=tblk, nsamp=nsamp),
+        functools.partial(pointing_body, tblk=tblk, nsamp=nsamp, per=per),
         grid_spec=grid_spec,
         out_shape=jax.ShapeDtypeStruct((dets, times, npix), jnp.float32),
     )(det_weight, pointing, picked, samples_row)

time: 164 us -> 164 us (level)
  no operation moved by 1% of the time
where the time goes in v7:
time: 164 us; the launch traced here: 163 us
  blocking collectives  34.4 us (21%)
  Pallas kernels  34.3 us (21%)
  local copies, waits for them, and re-layouts  30.2 us (18%)
  starting transfers between devices  25 us (15%)
  waiting for transfers between devices  21.4 us (13%)
  other arithmetic  12.1 us (7%)
  matrix products  4.12 us (3%)
    pallas_call x2, Pallas kernels, legendre_pallas(): pl.pallas_call(functools.partial(legendre_body, scale=math.sqrt(total_cyc...  18.6 us
    all_to_all x1, blocking collectives, on_device(): recv_b = lax.all_to_all(send_b, axes, 0, 0, tiled=True)  18.5 us
    all_to_all x1, blocking collectives, on_device(): recv_a = lax.all_to_all(send_a, axes, 0, 0, tiled=True)  15.9 us
    pallas_call x2, Pallas kernels, pointing_pallas(): pl.pallas_call(functools.partial(pointing_body, tblk=tblk, nsamp=nsamp, p...  15.8 us
    all_to_all x1, waiting for transfers between devices, on_device(): recv_b = lax.all_to_all(send_b, axes, 0, 0, tiled=True)  13.5 us
    all_to_all x1, starting transfers between devices, on_device(): info_recv = lax.all_to_all(info, axes, 0, 0, tiled=True)  11.5 us
    all_to_all x1, starting transfers between devices, on_device(): recv_b = lax.all_to_all(send_b, axes, 0, 0, tiled=True)  9.17 us
    all_to_all x1, waiting for transfers between devices, on_device(): info_recv = lax.all_to_all(info, axes, 0, 0, tiled=True)  7.27 us
  transfers between devices with their start and end apart: 3, of which 3 were waited for; matrix products, arithmetic and copies ran while one was open for 3% of the time, Pallas kernels for 6%

profile of v7, /device:TPU:1, one launch (start us, length us, event | category | flops | bytes accessed | tf_op | source)
XLA Modules:
  0.0 162.9 jit_solution(3265622852749328754)
XLA Ops:
  4.6 0.9 convolution_bitcast_fusion.3
  6.4 1.3 scatter_custom_fusion
  10.9 11.5 %all-to-all-start = ((f32[128,1,32]{2,1,0:T(1,128)}), f32[128,1,32]{2,1,0:T(1,128)S(1)}, u32[]{:S(2)}, u32[]{:S(2)}) async-start(f32[128,1,32]{2,1,0:T(1,128)} %bitcast.16), calls=%async_computation | async-start | bytes 131072 | tf_op jit(solution)/shard_map/all_to_all | solution.py:313
  23.6 1.3 dynamic_slice.3.m_ref
  25.0 7.3 %all-to-all-done = f32[128,1,32]{2,1,0:T(1,128)S(1)} async-done(((f32[128,1,32]{2,1,0:T(1,128)}), f32[128,1,32]{2,1,0:T(1,128)S(1)}, u32[]{:S(2)}, u32[]{:S(2)}) %all-to-all-start) | async-done | bytes 16416 | tf_op jit(solution)/shard_map/all_to_all | solution.py:313
  33.9 2.2 %reduce.13 = bf16[128,1024]{1,0:T(8,128)(2,1)S(1)} reduce(bf16[128,1,1024]{2,1,0:T(2,128)(2,1)S(1)} %all_to_all.52, bf16[]{:T(256)} %broadcast.932), dimensions={1}, to_apply=%all_to_all.52.reduce_sub_computation | reduce | bytes 524290 | tf_op jit(solution)/shard_map/all_to_all | solution.py:328
  37.0 4.3 %all-to-all-start.1 = ((bf16[128,2,512]{2,1,0:T(2,128)(2,1)}), bf16[128,2,512]{2,1,0:T(2,128)(2,1)S(1)}, u32[]{:S(2)}, u32[]{:S(2)}) async-start(bf16[128,2,512]{2,1,0:T(2,128)(2,1)} %reshape.1189), calls=%async_computation.1 | async-start | bytes 524288 | tf_op jit(solution)/shard_map/all_to_all | solution.py:328
  41.9 9.3 %shard_map.92 = f32[8,16,128]{2,1,0:T(8,128)} custom-call(s32[8]{0:T(128)} %dynamic_slice.3.m_ref, bf16[8,16,128]{2,1,0:T(8,128)(2,1)} %pad.7.coef_ref, f32[1,6144]{1,0:T(1,128)} %bitcast.205, bf16[8,6144,128]{2,1,0:T(8,128)(2,1)} %tab_ref.3), custom_call_target="tpu_custom_call" | custom-call | tf_op jit(solution)/shard_map/pallas_call | solution.py:170
  53.0 1.5 reduce.6
  54.6 1.5 gather_fusion
  56.1 7.9 %shard_map.91 = f32[4,64,128]{2,1,0:T(8,128)} custom-call(f32[4]{0:T(128)} %w_ref.3, bf16[4,64,128,128]{3,2,1,0:T(8,128)(2,1)} %p_ref.3, bf16[4,64,128]{2,1,0:T(8,128)(2,1)} %bitcast.198, f32[4,1,8192]{2,1,0:T(1,128)} %bitcast.191), custom_call_target="tpu_custom_call" | custom-call | tf_op jit(solution)/shard_map/pallas_call | solution.py:210
  64.0 1.6 %scatter_custom_fusion.1 = f32[1024,128]{1,0:T(8,128)S(1)} fusion(s32[256]{0:T(256)S(1)} %bitcast.215, f32[256,128]{1,0:T(8,128)} %bitcast.200, f32[]{:T(128)} %constant.129.clone.1), kind=kCustom, calls=%fused_computation.33 | custom fusion | bytes 524800 | tf_op jit(solution)/shard_map/scatter | solution.py:339
  65.7 1.4 copy.135
  67.2 9.2 %all-to-all-start.2 = ((f32[128,1,1040]{2,1,0:T(1,128)}), f32[128,1,1040]{2,1,0:T(1,128)S(1)}, u32[]{:S(2)}, u32[]{:S(2)}) async-start(f32[128,1,1040]{2,1,0:T(1,128)} %copy.135), calls=%async_computation.2 | async-start | bytes 1179648 | tf_op jit(solution)/shard_map/all_to_all | solution.py:346
  77.5 13.5 %all-to-all-done.2 = f32[128,1,1040]{2,1,0:T(1,128)S(1)} async-done(((f32[128,1,1040]{2,1,0:T(1,128)}), f32[128,1,1040]{2,1,0:T(1,128)S(1)}, u32[]{:S(2)}, u32[]{:S(2)}) %all-to-all-start.2) | async-done | bytes 532512 | tf_op jit(solution)/shard_map/all_to_all | solution.py:346
  91.1 0.9 copy.136
  99.6 15.9 %all_to_all.58 = bf16[128,2,520]{2,1,0:T(2,128)(2,1)S(1)} all-to-all(bf16[128,2,520]{2,1,0:T(2,128)(2,1)S(1)} %reshape.1191), channel_id=1, replica_groups=mesh['det'=8,'tm'=16] {'det','tm'}, dimensions={0} | all-to-all | bytes 532480 | tf_op jit(solution)/shard_map/all_to_all | solution.py:333
  116.0 0.9 copy.146
  117.2 1.5 gather_fusion.1
  119.3 9.3 %shard_map.94 = f32[8,16,128]{2,1,0:T(8,128)} custom-call(s32[8]{0:T(128)} %dynamic_slice.3.m_ref, bf16[8,16,128]{2,1,0:T(8,128)(2,1)} %pad.8.coef_ref, f32[1,6144]{1,0:T(1,128)} %bitcast.206, bf16[8,6144,128]{2,1,0:T(8,128)(2,1)} %tab_ref.3), custom_call_target="tpu_custom_call" | custom-call | tf_op jit(solution)/shard_map/pallas_call | solution.py:170
  129.5 7.9 %shard_map.93 = f32[4,64,128]{2,1,0:T(8,128)} custom-call(f32[4]{0:T(128)} %w_ref.3, bf16[4,64,128,128]{3,2,1,0:T(8,128)(2,1)} %p_ref.3, bf16[4,64,128]{2,1,0:T(8,128)(2,1)} %bitcast.197, f32[4,1,8192]{2,1,0:T(1,128)} %bitcast.192), custom_call_target="tpu_custom_call" | custom-call | tf_op jit(solution)/shard_map/pallas_call | solution.py:210
  137.4 1.9 %scatter_custom_fusion.2 = f32[1024,128]{1,0:T(8,128)S(1)} fusion(s32[256]{0:T(256)S(1)} %bitcast.216, f32[256,128]{1,0:T(8,128)} %bitcast.199, f32[]{:T(128)} %constant.129.clone.1), kind=kCustom, calls=%fused_computation.31 | custom fusion | bytes 524800 | tf_op jit(solution)/shard_map/scatter | solution.py:339
  140.0 18.5 %all_to_all.59 = f32[128,1,1040]{2,1,0:T(1,128)S(1)} all-to-all(f32[128,1,1040]{2,1,0:T(1,128)S(1)} %copy.151), channel_id=1, replica_groups=mesh['det'=8,'tm'=16] {'det','tm'}, dimensions={0} | all-to-all | bytes 1064960 | tf_op jit(solution)/shard_map/all_to_all | solution.py:346
  158.6 0.9 copy.152
  (144 shorter events, 29.1 us)
Async XLA Ops:
  10.9 21.3 %all-to-all-start = ((f32[128,1,32]{2,1,0:T(1,128)}), f32[128,1,32]{2,1,0:T(1,128)S(1)}, u32[]{:S(2)}, u32[]{:S(2)}) async-start(f32[128,1,32]{2,1,0:T(1,128)} %bitcast.16), calls=%async_computation | async-start | bytes 131072 | tf_op jit(solution)/shard_map/all_to_all | solution.py:313
  37.0 15.8 %all-to-all-start.1 = ((bf16[128,2,512]{2,1,0:T(2,128)(2,1)}), bf16[128,2,512]{2,1,0:T(2,128)(2,1)S(1)}, u32[]{:S(2)}, u32[]{:S(2)}) async-start(bf16[128,2,512]{2,1,0:T(2,128)(2,1)} %reshape.1189), calls=%async_computation.1 | async-start | bytes 524288 | tf_op jit(solution)/shard_map/all_to_all | solution.py:328
  51.2 41.9 %copy-start.1 = (s32[1024]{0:T(1024)S(1)}, s32[1024]{0:T(1024)}, u32[]{:S(2)}) copy-start(s32[1024]{0:T(1024)} %param.16) | copy-start | bytes 12292
  52.9 42.0 %copy-start = (f32[1,8192]{1,0:T(1,128)S(1)}, f32[1,8192]{1,0:T(1,128)}, u32[]{:S(2)}) copy-start(f32[1,8192]{1,0:T(1,128)} %param.13) | copy-start | bytes 98308
  67.2 23.9 %all-to-all-start.2 = ((f32[128,1,1040]{2,1,0:T(1,128)}), f32[128,1,1040]{2,1,0:T(1,128)S(1)}, u32[]{:S(2)}, u32[]{:S(2)}) async-start(f32[128,1,1040]{2,1,0:T(1,128)} %copy.135), calls=%async_computation.2 | async-start | bytes 1179648 | tf_op jit(solution)/shard_map/all_to_all | solution.py:346

commit v8 on v7

--- a/solution.py
+++ b/solution.py
@@ -12,7 +12,7 @@
 ITERS = 2
 
 
-highest = lax.Precision.HIGHEST
+highest = lax.Precision.HIGH
 
 
 def phase_pair(first_len, second_len, length, sign):

time: 164 us -> 163 us (level)
  no operation moved by 1% of the time
where the time goes in v8:
time: 163 us; the launch traced here: 162 us
  blocking collectives  34.4 us (21%)
  Pallas kernels  34.3 us (21%)
  local copies, waits for them, and re-layouts  29.9 us (18%)
  starting transfers between devices  25 us (15%)
  waiting for transfers between devices  21.4 us (13%)
  other arithmetic  12.1 us (7%)
  matrix products  3.67 us (2%)
    pallas_call x2, Pallas kernels, legendre_pallas(): pl.pallas_call(functools.partial(legendre_body, scale=math.sqrt(total_cyc...  18.6 us
    all_to_all x1, blocking collectives, on_device(): recv_b = lax.all_to_all(send_b, axes, 0, 0, tiled=True)  18.5 us
    all_to_all x1, blocking collectives, on_device(): recv_a = lax.all_to_all(send_a, axes, 0, 0, tiled=True)  15.9 us
    pallas_call x2, Pallas kernels, pointing_pallas(): pl.pallas_call(functools.partial(pointing_body, tblk=tblk, nsamp=nsamp, p...  15.8 us
    all_to_all x1, waiting for transfers between devices, on_device(): recv_b = lax.all_to_all(send_b, axes, 0, 0, tiled=True)  13.5 us
    all_to_all x1, starting transfers between devices, on_device(): info_recv = lax.all_to_all(info, axes, 0, 0, tiled=True)  11.5 us
    all_to_all x1, starting transfers between devices, on_device(): recv_b = lax.all_to_all(send_b, axes, 0, 0, tiled=True)  9.18 us
    all_to_all x1, waiting for transfers between devices, on_device(): info_recv = lax.all_to_all(info, axes, 0, 0, tiled=True)  7.27 us
  transfers between devices with their start and end apart: 3, of which 3 were waited for; matrix products, arithmetic and copies ran while one was open for 3% of the time, Pallas kernels for 6%

profile of v8, /device:TPU:1, one launch (start us, length us, event | category | flops | bytes accessed | tf_op | source)
XLA Modules:
  0.0 162.2 jit_solution(14615250840708001594)
XLA Ops:
  4.6 0.9 convolution_bitcast_fusion.3
  6.3 1.3 scatter_custom_fusion
  10.9 11.5 %all-to-all-start = ((f32[128,1,32]{2,1,0:T(1,128)}), f32[128,1,32]{2,1,0:T(1,128)S(1)}, u32[]{:S(2)}, u32[]{:S(2)}) async-start(f32[128,1,32]{2,1,0:T(1,128)} %bitcast.16), calls=%async_computation | async-start | bytes 131072 | tf_op jit(solution)/shard_map/all_to_all | solution.py:313
  23.5 1.3 dynamic_slice.3.m_ref
  24.9 7.3 %all-to-all-done = f32[128,1,32]{2,1,0:T(1,128)S(1)} async-done(((f32[128,1,32]{2,1,0:T(1,128)}), f32[128,1,32]{2,1,0:T(1,128)S(1)}, u32[]{:S(2)}, u32[]{:S(2)}) %all-to-all-start) | async-done | bytes 16416 | tf_op jit(solution)/shard_map/all_to_all | solution.py:313
  33.8 2.2 %reduce.13 = bf16[128,1024]{1,0:T(8,128)(2,1)S(1)} reduce(bf16[128,1,1024]{2,1,0:T(2,128)(2,1)S(1)} %all_to_all.52, bf16[]{:T(256)} %broadcast.932), dimensions={1}, to_apply=%all_to_all.52.reduce_sub_computation | reduce | bytes 524290 | tf_op jit(solution)/shard_map/all_to_all | solution.py:328
  36.9 4.3 %all-to-all-start.1 = ((bf16[128,2,512]{2,1,0:T(2,128)(2,1)}), bf16[128,2,512]{2,1,0:T(2,128)(2,1)S(1)}, u32[]{:S(2)}, u32[]{:S(2)}) async-start(bf16[128,2,512]{2,1,0:T(2,128)(2,1)} %reshape.1189), calls=%async_computation.1 | async-start | bytes 524288 | tf_op jit(solution)/shard_map/all_to_all | solution.py:328
  41.8 9.3 %shard_map.92 = f32[8,16,128]{2,1,0:T(8,128)} custom-call(s32[8]{0:T(128)} %dynamic_slice.3.m_ref, bf16[8,16,128]{2,1,0:T(8,128)(2,1)} %pad.7.coef_ref, f32[1,6144]{1,0:T(1,128)} %bitcast.205, bf16[8,6144,128]{2,1,0:T(8,128)(2,1)} %tab_ref.3), custom_call_target="tpu_custom_call" | custom-call | tf_op jit(solution)/shard_map/pallas_call | solution.py:170
  52.9 1.5 reduce.6
  54.5 1.5 gather_fusion
  56.0 7.9 %shard_map.91 = f32[4,64,128]{2,1,0:T(8,128)} custom-call(f32[4]{0:T(128)} %w_ref.3, bf16[4,64,128,128]{3,2,1,0:T(8,128)(2,1)} %p_ref.3, bf16[4,64,128]{2,1,0:T(8,128)(2,1)} %bitcast.198, f32[4,1,8192]{2,1,0:T(1,128)} %bitcast.191), custom_call_target="tpu_custom_call" | custom-call | tf_op jit(solution)/shard_map/pallas_call | solution.py:210
  63.9 1.6 %scatter_custom_fusion.1 = f32[1024,128]{1,0:T(8,128)S(1)} fusion(s32[256]{0:T(256)S(1)} %bitcast.215, f32[256,128]{1,0:T(8,128)} %bitcast.200, f32[]{:T(128)} %constant.129.clone.1), kind=kCustom, calls=%fused_computation.33 | custom fusion | bytes 524800 | tf_op jit(solution)/shard_map/scatter | solution.py:339
  65.7 1.4 copy.135
  67.1 9.2 %all-to-all-start.2 = ((f32[128,1,1040]{2,1,0:T(1,128)}), f32[128,1,1040]{2,1,0:T(1,128)S(1)}, u32[]{:S(2)}, u32[]{:S(2)}) async-start(f32[128,1,1040]{2,1,0:T(1,128)} %copy.135), calls=%async_computation.2 | async-start | bytes 1179648 | tf_op jit(solution)/shard_map/all_to_all | solution.py:346
  77.5 13.5 %all-to-all-done.2 = f32[128,1,1040]{2,1,0:T(1,128)S(1)} async-done(((f32[128,1,1040]{2,1,0:T(1,128)}), f32[128,1,1040]{2,1,0:T(1,128)S(1)}, u32[]{:S(2)}, u32[]{:S(2)}) %all-to-all-start.2) | async-done | bytes 532512 | tf_op jit(solution)/shard_map/all_to_all | solution.py:346
  91.0 0.9 copy.136
  99.3 15.9 %all_to_all.58 = bf16[128,2,520]{2,1,0:T(2,128)(2,1)S(1)} all-to-all(bf16[128,2,520]{2,1,0:T(2,128)(2,1)S(1)} %reshape.1191), channel_id=1, replica_groups=mesh['det'=8,'tm'=16] {'det','tm'}, dimensions={0} | all-to-all | bytes 532480 | tf_op jit(solution)/shard_map/all_to_all | solution.py:333
  115.7 0.9 copy.146
  116.9 1.5 gather_fusion.1
  119.0 9.3 %shard_map.94 = f32[8,16,128]{2,1,0:T(8,128)} custom-call(s32[8]{0:T(128)} %dynamic_slice.3.m_ref, bf16[8,16,128]{2,1,0:T(8,128)(2,1)} %pad.8.coef_ref, f32[1,6144]{1,0:T(1,128)} %bitcast.206, bf16[8,6144,128]{2,1,0:T(8,128)(2,1)} %tab_ref.3), custom_call_target="tpu_custom_call" | custom-call | tf_op jit(solution)/shard_map/pallas_call | solution.py:170
  129.2 7.9 %shard_map.93 = f32[4,64,128]{2,1,0:T(8,128)} custom-call(f32[4]{0:T(128)} %w_ref.3, bf16[4,64,128,128]{3,2,1,0:T(8,128)(2,1)} %p_ref.3, bf16[4,64,128]{2,1,0:T(8,128)(2,1)} %bitcast.197, f32[4,1,8192]{2,1,0:T(1,128)} %bitcast.192), custom_call_target="tpu_custom_call" | custom-call | tf_op jit(solution)/shard_map/pallas_call | solution.py:210
  137.1 1.6 %scatter_custom_fusion.2 = f32[1024,128]{1,0:T(8,128)S(1)} fusion(s32[256]{0:T(256)S(1)} %bitcast.216, f32[256,128]{1,0:T(8,128)} %bitcast.199, f32[]{:T(128)} %constant.129.clone.1), kind=kCustom, calls=%fused_computation.31 | custom fusion | bytes 524800 | tf_op jit(solution)/shard_map/scatter | solution.py:339
  139.5 18.5 %all_to_all.59 = f32[128,1,1040]{2,1,0:T(1,128)S(1)} all-to-all(f32[128,1,1040]{2,1,0:T(1,128)S(1)} %copy.151), channel_id=1, replica_groups=mesh['det'=8,'tm'=16] {'det','tm'}, dimensions={0} | all-to-all | bytes 1064960 | tf_op jit(solution)/shard_map/all_to_all | solution.py:346
  158.0 0.9 copy.152
  (144 shorter events, 28.7 us)
Async XLA Ops:
  10.9 21.3 %all-to-all-start = ((f32[128,1,32]{2,1,0:T(1,128)}), f32[128,1,32]{2,1,0:T(1,128)S(1)}, u32[]{:S(2)}, u32[]{:S(2)}) async-start(f32[128,1,32]{2,1,0:T(1,128)} %bitcast.16), calls=%async_computation | async-start | bytes 131072 | tf_op jit(solution)/shard_map/all_to_all | solution.py:313
  36.9 15.8 %all-to-all-start.1 = ((bf16[128,2,512]{2,1,0:T(2,128)(2,1)}), bf16[128,2,512]{2,1,0:T(2,128)(2,1)S(1)}, u32[]{:S(2)}, u32[]{:S(2)}) async-start(bf16[128,2,512]{2,1,0:T(2,128)(2,1)} %reshape.1189), calls=%async_computation.1 | async-start | bytes 524288 | tf_op jit(solution)/shard_map/all_to_all | solution.py:328
  51.1 41.8 %copy-start.1 = (s32[1024]{0:T(1024)S(1)}, s32[1024]{0:T(1024)}, u32[]{:S(2)}) copy-start(s32[1024]{0:T(1024)} %param.16) | copy-start | bytes 12292
  52.9 41.8 %copy-start = (f32[1,8192]{1,0:T(1,128)S(1)}, f32[1,8192]{1,0:T(1,128)}, u32[]{:S(2)}) copy-start(f32[1,8192]{1,0:T(1,128)} %param.13) | copy-start | bytes 98308
  67.1 23.9 %all-to-all-start.2 = ((f32[128,1,1040]{2,1,0:T(1,128)}), f32[128,1,1040]{2,1,0:T(1,128)S(1)}, u32[]{:S(2)}, u32[]{:S(2)}) async-start(f32[128,1,1040]{2,1,0:T(1,128)} %copy.135), calls=%async_computation.2 | async-start | bytes 1179648 | tf_op jit(solution)/shard_map/all_to_all | solution.py:346

commit v9 on v7

--- a/solution.py
+++ b/solution.py
@@ -345,7 +345,15 @@
         )
         recv_b = lax.all_to_all(send_b, axes, 0, 0, tiled=True)
         binned_in = recv_b[:, : CAP * 128].reshape(slots, 128)
-        binned = jnp.dot(want_hot, binned_in, precision=highest).reshape(cycles_here, length)
+        piece_hi = binned_in.astype(jnp.bfloat16)
+        rest = binned_in - piece_hi.astype(jnp.float32)
+        piece_mid = rest.astype(jnp.bfloat16)
+        piece_lo = (rest - piece_mid.astype(jnp.float32)).astype(jnp.bfloat16)
+        hot_half = want_hot.astype(jnp.bfloat16)
+        binned = sum(
+            jnp.dot(hot_half, piece, preferred_element_type=jnp.float32)
+            for piece in (piece_lo, piece_mid, piece_hi)
+        ).reshape(cycles_here, length)
         returned = recv_b[:, CAP * 128 :].reshape(owners, 2, count_here, cycles_here)
         returned = returned.transpose(1, 0, 2, 3).reshape(2, owners * count_here, cycles_here)
         filtered = spectrum_back(

time: 164 us -> 164 us (level)
  no operation moved by 1% of the time
where the time goes in v9:
time: 164 us; the launch traced here: 163 us
  Pallas kernels  34.5 us (21%)
  blocking collectives  34.4 us (21%)
  local copies, waits for them, and re-layouts  30.2 us (18%)
  starting transfers between devices  25 us (15%)
  waiting for transfers between devices  21.4 us (13%)
  other arithmetic  12.1 us (7%)
  matrix products  4.55 us (3%)
    pallas_call x2, Pallas kernels, legendre_pallas(): pl.pallas_call(functools.partial(legendre_body, scale=math.sqrt(total_cyc...  18.6 us
    all_to_all x1, blocking collectives, on_device(): recv_b = lax.all_to_all(send_b, axes, 0, 0, tiled=True)  18.5 us
    pallas_call x2, Pallas kernels, pointing_pallas(): pl.pallas_call(functools.partial(pointing_body, tblk=tblk, nsamp=nsamp, p...  15.9 us
    all_to_all x1, blocking collectives, on_device(): recv_a = lax.all_to_all(send_a, axes, 0, 0, tiled=True)  15.9 us
    all_to_all x1, waiting for transfers between devices, on_device(): recv_b = lax.all_to_all(send_b, axes, 0, 0, tiled=True)  13.5 us
    all_to_all x1, starting transfers between devices, on_device(): info_recv = lax.all_to_all(info, axes, 0, 0, tiled=True)  11.5 us
    all_to_all x1, starting transfers between devices, on_device(): recv_b = lax.all_to_all(send_b, axes, 0, 0, tiled=True)  9.18 us
    all_to_all x1, waiting for transfers between devices, on_device(): info_recv = lax.all_to_all(info, axes, 0, 0, tiled=True)  7.27 us
  transfers between devices with their start and end apart: 3, of which 3 were waited for; matrix products, arithmetic and copies ran while one was open for 3% of the time, Pallas kernels for 6%

profile of v9, /device:TPU:1, one launch (start us, length us, event | category | flops | bytes accessed | tf_op | source)
XLA Modules:
  0.0 163.5 jit_solution(10762737093459622961)
XLA Ops:
  4.6 0.9 convolution_bitcast_fusion.3
  6.4 1.3 scatter_custom_fusion
  10.9 11.5 %all-to-all-start = ((f32[128,1,32]{2,1,0:T(1,128)}), f32[128,1,32]{2,1,0:T(1,128)S(1)}, u32[]{:S(2)}, u32[]{:S(2)}) async-start(f32[128,1,32]{2,1,0:T(1,128)} %bitcast.16), calls=%async_computation | async-start | bytes 131072 | tf_op jit(solution)/shard_map/all_to_all | solution.py:313
  23.6 1.3 dynamic_slice.3.m_ref
  25.0 7.3 %all-to-all-done = f32[128,1,32]{2,1,0:T(1,128)S(1)} async-done(((f32[128,1,32]{2,1,0:T(1,128)}), f32[128,1,32]{2,1,0:T(1,128)S(1)}, u32[]{:S(2)}, u32[]{:S(2)}) %all-to-all-start) | async-done | bytes 16416 | tf_op jit(solution)/shard_map/all_to_all | solution.py:313
  33.9 2.2 %reduce.13 = bf16[128,1024]{1,0:T(8,128)(2,1)S(1)} reduce(bf16[128,1,1024]{2,1,0:T(2,128)(2,1)S(1)} %all_to_all.52, bf16[]{:T(256)} %broadcast.932), dimensions={1}, to_apply=%all_to_all.52.reduce_sub_computation | reduce | bytes 524290 | tf_op jit(solution)/shard_map/all_to_all | solution.py:328
  37.0 4.3 %all-to-all-start.1 = ((bf16[128,2,512]{2,1,0:T(2,128)(2,1)}), bf16[128,2,512]{2,1,0:T(2,128)(2,1)S(1)}, u32[]{:S(2)}, u32[]{:S(2)}) async-start(bf16[128,2,512]{2,1,0:T(2,128)(2,1)} %reshape.1189), calls=%async_computation.1 | async-start | bytes 524288 | tf_op jit(solution)/shard_map/all_to_all | solution.py:328
  41.9 9.3 %shard_map.92 = f32[8,16,128]{2,1,0:T(8,128)} custom-call(s32[8]{0:T(128)} %dynamic_slice.3.m_ref, bf16[8,16,128]{2,1,0:T(8,128)(2,1)} %pad.7.coef_ref, f32[1,6144]{1,0:T(1,128)} %bitcast.203, bf16[8,6144,128]{2,1,0:T(8,128)(2,1)} %tab_ref.3), custom_call_target="tpu_custom_call" | custom-call | tf_op jit(solution)/shard_map/pallas_call | solution.py:170
  52.9 1.5 reduce.6
  54.6 1.5 gather_fusion
  56.1 8.0 %shard_map.91 = f32[4,64,128]{2,1,0:T(8,128)} custom-call(f32[4]{0:T(128)} %w_ref.3, bf16[4,64,128,128]{3,2,1,0:T(8,128)(2,1)} %p_ref.3, bf16[4,64,128]{2,1,0:T(8,128)(2,1)} %bitcast.196, f32[4,1,8192]{2,1,0:T(1,128)} %bitcast.189), custom_call_target="tpu_custom_call" | custom-call | tf_op jit(solution)/shard_map/pallas_call | solution.py:210
  64.1 1.6 %scatter_custom_fusion.1 = f32[1024,128]{1,0:T(8,128)S(1)} fusion(s32[256]{0:T(256)S(1)} %bitcast.213, f32[256,128]{1,0:T(8,128)} %bitcast.198, f32[]{:T(128)} %constant.129.clone.1), kind=kCustom, calls=%fused_computation.47 | custom fusion | bytes 524800 | tf_op jit(solution)/shard_map/scatter | solution.py:339
  65.9 1.4 copy.135
  67.3 9.2 %all-to-all-start.2 = ((f32[128,1,1040]{2,1,0:T(1,128)}), f32[128,1,1040]{2,1,0:T(1,128)S(1)}, u32[]{:S(2)}, u32[]{:S(2)}) async-start(f32[128,1,1040]{2,1,0:T(1,128)} %copy.135), calls=%async_computation.2 | async-start | bytes 1179648 | tf_op jit(solution)/shard_map/all_to_all | solution.py:346
  77.7 13.5 %all-to-all-done.2 = f32[128,1,1040]{2,1,0:T(1,128)S(1)} async-done(((f32[128,1,1040]{2,1,0:T(1,128)}), f32[128,1,1040]{2,1,0:T(1,128)S(1)}, u32[]{:S(2)}, u32[]{:S(2)}) %all-to-all-start.2) | async-done | bytes 532512 | tf_op jit(solution)/shard_map/all_to_all | solution.py:346
  91.2 0.9 copy.136
  99.9 15.9 %all_to_all.58 = bf16[128,2,520]{2,1,0:T(2,128)(2,1)S(1)} all-to-all(bf16[128,2,520]{2,1,0:T(2,128)(2,1)S(1)} %reshape.1191), channel_id=1, replica_groups=mesh['det'=8,'tm'=16] {'det','tm'}, dimensions={0} | all-to-all | bytes 532480 | tf_op jit(solution)/shard_map/all_to_all | solution.py:333
  116.3 0.9 copy.146
  117.6 1.5 gather_fusion.1
  119.7 9.3 %shard_map.94 = f32[8,16,128]{2,1,0:T(8,128)} custom-call(s32[8]{0:T(128)} %dynamic_slice.3.m_ref, bf16[8,16,128]{2,1,0:T(8,128)(2,1)} %pad.8.coef_ref, f32[1,6144]{1,0:T(1,128)} %bitcast.204, bf16[8,6144,128]{2,1,0:T(8,128)(2,1)} %tab_ref.3), custom_call_target="tpu_custom_call" | custom-call | tf_op jit(solution)/shard_map/pallas_call | solution.py:170
  129.8 7.9 %shard_map.93 = f32[4,64,128]{2,1,0:T(8,128)} custom-call(f32[4]{0:T(128)} %w_ref.3, bf16[4,64,128,128]{3,2,1,0:T(8,128)(2,1)} %p_ref.3, bf16[4,64,128]{2,1,0:T(8,128)(2,1)} %bitcast.195, f32[4,1,8192]{2,1,0:T(1,128)} %bitcast.190), custom_call_target="tpu_custom_call" | custom-call | tf_op jit(solution)/shard_map/pallas_call | solution.py:210
  137.7 1.9 %scatter_custom_fusion.2 = f32[1024,128]{1,0:T(8,128)S(1)} fusion(s32[256]{0:T(256)S(1)} %bitcast.214, f32[256,128]{1,0:T(8,128)} %bitcast.197, f32[]{:T(128)} %constant.129.clone.1), kind=kCustom, calls=%fused_computation.45 | custom fusion | bytes 524800 | tf_op jit(solution)/shard_map/scatter | solution.py:339
  140.4 18.5 %all_to_all.59 = f32[128,1,1040]{2,1,0:T(1,128)S(1)} all-to-all(f32[128,1,1040]{2,1,0:T(1,128)S(1)} %copy.151), channel_id=1, replica_groups=mesh['det'=8,'tm'=16] {'det','tm'}, dimensions={0} | all-to-all | bytes 1064960 | tf_op jit(solution)/shard_map/all_to_all | solution.py:346
  158.9 0.9 copy.152
  (148 shorter events, 29.6 us)
Async XLA Ops:
  10.9 21.3 %all-to-all-start = ((f32[128,1,32]{2,1,0:T(1,128)}), f32[128,1,32]{2,1,0:T(1,128)S(1)}, u32[]{:S(2)}, u32[]{:S(2)}) async-start(f32[128,1,32]{2,1,0:T(1,128)} %bitcast.16), calls=%async_computation | async-start | bytes 131072 | tf_op jit(solution)/shard_map/all_to_all | solution.py:313
  37.0 15.8 %all-to-all-start.1 = ((bf16[128,2,512]{2,1,0:T(2,128)(2,1)}), bf16[128,2,512]{2,1,0:T(2,128)(2,1)S(1)}, u32[]{:S(2)}, u32[]{:S(2)}) async-start(bf16[128,2,512]{2,1,0:T(2,128)(2,1)} %reshape.1189), calls=%async_computation.1 | async-start | bytes 524288 | tf_op jit(solution)/shard_map/all_to_all | solution.py:328
  51.2 42.2 %copy-start.1 = (s32[1024]{0:T(1024)S(1)}, s32[1024]{0:T(1024)}, u32[]{:S(2)}) copy-start(s32[1024]{0:T(1024)} %param.16) | copy-start | bytes 12292
  56.1 39.2 %copy-start = (f32[1,8192]{1,0:T(1,128)S(1)}, f32[1,8192]{1,0:T(1,128)}, u32[]{:S(2)}) copy-start(f32[1,8192]{1,0:T(1,128)} %param.13) | copy-start | bytes 98308
  67.3 23.9 %all-to-all-start.2 = ((f32[128,1,1040]{2,1,0:T(1,128)}), f32[128,1,1040]{2,1,0:T(1,128)S(1)}, u32[]{:S(2)}, u32[]{:S(2)}) async-start(f32[128,1,1040]{2,1,0:T(1,128)} %copy.135), calls=%async_computation.2 | async-start | bytes 1179648 | tf_op jit(solution)/shard_map/all_to_all | solution.py:346
